TPU v7x, 256 devices: a whole 4x4x8 slice. The times are simulated.
256 devices in a mesh: dp: 32 (over z, x_hi, core), tm: 8 (over y, x_lo).
Axes of the slice: x: 4 (x_hi: 2, x_lo: 2; x = x_hi * 2 + x_lo), y: 4, z: 8, core: 2. Of those that a mesh axis runs over, the one named last changes fastest.
Arguments:
- queries: bfloat16 [32, 3072, 256], P('dp', 'tm'), may hold values from -6 to 6
- key_input: bfloat16 [32, 3072, 256], P('dp', 'tm'), may hold values from -6 to 6
- value_input: bfloat16 [32, 3072, 256], P('dp', 'tm'), may hold values from -6 to 6
- lengths: int32 [32], P('dp'), may hold values from 1536 to 3072, as said below
- projection: bfloat16 [4096, 256], P('dp'), may hold values from -0.09375 to 0.09375
- upstream: bfloat16 [32, 3072, 4096], P('dp', 'tm'), may hold values from -6 to 6
- glu_input: bfloat16 [32, 3072, 4096], P('dp', 'tm'), may hold values from -6 to 6
- kernel: bfloat16 [2048, 31], P('dp'), may hold values from -1 to 1
- norm_gain: bfloat16 [2048], P('dp'), may hold values from 0.5 to 1.5
- conv_upstream: bfloat16 [32, 3072, 2048], P('dp', 'tm'), may hold values from -6 to 6
Outputs:
- grad_queries: bfloat16 [32, 3072, 256], P('dp', 'tm')
- grad_keys: bfloat16 [32, 3072, 256], P('dp', 'tm')
- grad_values: bfloat16 [32, 3072, 256], P('dp', 'tm')
- grad_projection: bfloat16 [4096, 256], P('dp')
- grad_glu: bfloat16 [32, 3072, 4096], P('dp', 'tm')
- grad_kernel: float32 [2048, 31], P('dp')
- grad_gain: float32 [2048], P('dp')
Inputs may be any that keep to these rules, and one draw needn't show every extreme that they name: `lengths`: the valid frames of an utterance are its first ones; one utterance has all 3072 valid and one exactly 1536.
All inputs are finite; a program needn't handle non-finite values.
Results may differ from a plain program's by a relative error of at most 0.02.
Values may be sent and summed in bfloat16 or wider, within the bound.
No kernel may reach another device: no remote copies, remote signals or barrier semaphores. Data moves between devices by JAX's collectives and lax.ppermute only.
A program may use at most 128 MiB of HBM per device.

v0:
```python
import jax
import jax.numpy as jnp
from jax import lax
from jax.sharding import PartitionSpec as P

HEADS = 2
HDIM = 128
CH = 2048
KW = 31


NEG_FILL = -1e30
NORM_EPS = 1e-05


def from_behind(block, axis, distance):
    devices = range(lax.axis_size(axis))
    route = [((i - distance) % len(devices), i) for i in devices]
    return lax.ppermute(block, axis, route)


def extended(cells, sides, width):
    for axis, dim in sides:
        count = lax.axis_size(axis)
        ends = count - 1
        head = lax.slice_in_dim(cells, 0, width, axis=dim)
        tail = lax.slice_in_dim(cells, cells.shape[dim] - width, cells.shape[dim], axis=dim)
        cells = jnp.concatenate(
            [
                lax.ppermute(tail, axis, [(i, (i + 1) % count) for i in range(ends)]),
                cells,
                lax.ppermute(head, axis, [((i + 1) % count, i) for i in range(ends)]),
            ],
            axis=dim,
        )
    return cells


def depthwise(padded, kernel_f, frame_rows):
    mixed = jnp.zeros((frame_rows, kernel_f.shape[0]), jnp.float32)
    for tap in range(kernel_f.shape[1]):
        mixed = mixed + padded[tap : tap + frame_rows].astype(jnp.float32) * kernel_f[:, tap]
    return mixed


def back_depthwise(grad_pad, kernel_f, frame_rows):
    half_width = (kernel_f.shape[1] - 1) // 2
    result = jnp.zeros((frame_rows, kernel_f.shape[0]), jnp.float32)
    for tap in range(kernel_f.shape[1]):
        begin = 2 * half_width - tap
        result = (
            result + grad_pad[begin : begin + frame_rows].astype(jnp.float32) * kernel_f[:, tap]
        )
    return result


def tap_products(grad_low, padded, frame_rows, tap_count):
    grad_f = grad_low.astype(jnp.float32)
    return jnp.stack(
        [
            jnp.sum(grad_f * padded[tap : tap + frame_rows].astype(jnp.float32), axis=0)
            for tap in range(tap_count)
        ],
        axis=1,
    )


def norm_backward(mixed, gain_f, cotangent, frame_live):
    centre = mixed - jnp.mean(mixed, axis=-1, keepdims=True)
    inv_std = lax.rsqrt(jnp.mean(centre * centre, axis=-1, keepdims=True) + NORM_EPS)
    standard = centre * inv_std
    normed = standard * gain_f
    squash = jax.nn.sigmoid(normed)
    grad_normed = (
        cotangent.astype(jnp.float32) * frame_live * (squash + normed * squash * (1.0 - squash))
    )
    gain_term = jnp.sum(grad_normed * standard, axis=0)
    scaled = grad_normed * gain_f
    grad_conv = inv_std * (
        scaled
        - jnp.mean(scaled, axis=-1, keepdims=True)
        - standard * jnp.mean(scaled * standard, axis=-1, keepdims=True)
    )
    return (grad_conv.astype(jnp.bfloat16), gain_term)


def per_device(
    queries,
    key_input,
    value_input,
    lengths,
    projection,
    upstream,
    glu_input,
    kernel,
    norm_gain,
    conv_upstream,
):
    time_count = lax.axis_size("tm")
    time_rank = lax.axis_index("tm")
    frame_rows = queries.shape[1]
    flat_width = queries.shape[2]
    score_scale = HDIM ** (-0.5)
    length = lengths[0]
    full_proj, full_kernel, full_gain = (
        lax.all_gather(projection, "dp", axis=0, tiled=True),
        lax.all_gather(kernel, "dp", axis=0, tiled=True),
        lax.all_gather(norm_gain, "dp", axis=0, tiled=True),
    )
    query_heads = queries[0].reshape(frame_rows, HEADS, HDIM)
    key_heads = key_input[0].reshape(frame_rows, HEADS, HDIM)
    value_heads = value_input[0].reshape(frame_rows, HEADS, HDIM)

    def block_scores(key_block, key_offset):
        scores = (
            jnp.einsum("qhd,khd->hqk", query_heads, key_block, preferred_element_type=jnp.float32)
            * score_scale
        )
        key_live = key_offset + jnp.arange(key_block.shape[0], dtype=jnp.int32) < length
        return jnp.where(key_live[None, None, :], scores, NEG_FILL)

    def absorb(state_now, key_block, value_block, key_offset):
        run_top, run_total, run_acc = state_now
        scores = block_scores(key_block, key_offset)
        new_top = jnp.maximum(run_top, jnp.max(scores, axis=-1))
        factor = jnp.exp(run_top - new_top)
        weights = jnp.exp(scores - new_top[:, :, None])
        run_total = run_total * factor + jnp.sum(weights, axis=-1)
        contrib = jnp.einsum(
            "hqk,khd->qhd",
            weights,
            value_block.astype(jnp.float32),
            precision=lax.Precision.HIGHEST,
        )
        run_acc = run_acc * jnp.transpose(factor)[:, :, None] + contrib
        return (new_top, run_total, run_acc)

    start_state = (
        jnp.full((HEADS, frame_rows), NEG_FILL, jnp.float32),
        jnp.zeros((HEADS, frame_rows), jnp.float32),
        jnp.zeros((frame_rows, HEADS, HDIM), jnp.float32),
    )

    def forward_step(step, loop_state):
        key_block, value_block, inner = loop_state
        source = (time_rank - step) % time_count
        inner = absorb(inner, key_block, value_block, source * frame_rows)
        key_block, value_block = from_behind((key_block, value_block), "tm", 1)
        return (key_block, value_block, inner)

    key_block, value_block, inner = lax.fori_loop(
        0, time_count - 1, forward_step, (key_heads, value_heads, start_state)
    )
    source = (time_rank - (time_count - 1)) % time_count
    state_now = absorb(inner, key_block, value_block, source * frame_rows)
    run_top, run_total, run_acc = state_now
    log_total = run_top + jnp.log(run_total)
    attended = (run_acc / jnp.transpose(run_total)[:, :, None]).astype(jnp.bfloat16)
    upstream_rows = upstream[0]
    grad_out = jnp.dot(upstream_rows, full_proj, preferred_element_type=jnp.float32).astype(
        jnp.bfloat16
    )
    grad_heads = grad_out.reshape(frame_rows, HEADS, HDIM)
    row_delta = jnp.einsum("qhd,qhd->hq", grad_heads, attended, preferred_element_type=jnp.float32)

    def backward_block(key_block, value_block, key_offset):
        scores = block_scores(key_block, key_offset)
        weights = jnp.exp(scores - log_total[:, :, None])
        weights_low = weights.astype(jnp.bfloat16)
        add_value = jnp.einsum(
            "hqk,qhd->khd", weights_low, grad_heads, preferred_element_type=jnp.float32
        )
        grad_weights = jnp.einsum(
            "qhd,khd->hqk", grad_heads, value_block, preferred_element_type=jnp.float32
        )
        grad_scores = (weights * (grad_weights - row_delta[:, :, None]) * score_scale).astype(
            jnp.bfloat16
        )
        add_query = jnp.einsum(
            "hqk,khd->qhd", grad_scores, key_block, preferred_element_type=jnp.float32
        )
        add_key = jnp.einsum(
            "hqk,qhd->khd", grad_scores, query_heads, preferred_element_type=jnp.float32
        )
        return (add_query, add_key, add_value)

    zero_heads = jnp.zeros((frame_rows, HEADS, HDIM), jnp.float32)

    def pass_grads(key_acc, value_acc):
        return from_behind((key_acc, value_acc), "tm", 1)

    def backward_step(step, loop_state):
        key_block, value_block, key_acc, value_acc, query_acc = loop_state
        source = (time_rank - step) % time_count
        add_query, add_key, add_value = backward_block(key_block, value_block, source * frame_rows)
        key_acc, value_acc = pass_grads(key_acc + add_key, value_acc + add_value)
        key_block, value_block = from_behind((key_block, value_block), "tm", 1)
        return (key_block, value_block, key_acc, value_acc, query_acc + add_query)

    key_block, value_block, key_acc, value_acc, query_acc = lax.fori_loop(
        0,
        time_count - 1,
        backward_step,
        (key_heads, value_heads, zero_heads, zero_heads, zero_heads),
    )
    source = (time_rank - (time_count - 1)) % time_count
    add_query, add_key, add_value = backward_block(key_block, value_block, source * frame_rows)
    key_acc, value_acc = pass_grads(key_acc + add_key, value_acc + add_value)
    query_acc = query_acc + add_query
    grad_queries = query_acc.reshape(1, frame_rows, flat_width).astype(jnp.bfloat16)
    grad_keys = key_acc.reshape(1, frame_rows, flat_width).astype(jnp.bfloat16)
    grad_values = value_acc.reshape(1, frame_rows, flat_width).astype(jnp.bfloat16)
    half_width = (KW - 1) // 2
    frame_ids = time_rank * frame_rows + jnp.arange(frame_rows, dtype=jnp.int32)
    frame_live = (frame_ids < length).astype(jnp.float32)[:, None]
    glu_rows = glu_input[0]
    linear = glu_rows[:, :CH].astype(jnp.float32)
    gate_sig = jax.nn.sigmoid(glu_rows[:, CH:].astype(jnp.float32))
    activ = (linear * gate_sig * frame_live).astype(jnp.bfloat16)
    padded = extended(activ, (("tm", 0),), half_width)
    kernel_f = full_kernel.astype(jnp.float32)
    gain_f = full_gain.astype(jnp.float32)
    mixed = depthwise(padded, kernel_f, frame_rows)
    grad_conv, gain_term = norm_backward(mixed, gain_f, conv_upstream[0], frame_live)
    grad_pad = extended(grad_conv, (("tm", 0),), half_width)
    kernel_term = tap_products(grad_conv, padded, frame_rows, KW)
    grad_activ = back_depthwise(grad_pad, kernel_f, frame_rows) * frame_live
    first_half = grad_activ * gate_sig
    second_half = grad_activ * linear * gate_sig * (1.0 - gate_sig)
    grad_glu = jnp.concatenate([first_half, second_half], axis=-1).astype(jnp.bfloat16)[None]
    attended_flat = attended.reshape(frame_rows, flat_width)
    proj_part = lax.psum_scatter(
        lax.dot_general(
            upstream_rows,
            attended_flat,
            (((0,), (0,)), ((), ())),
            preferred_element_type=jnp.float32,
        ),
        "dp",
        scatter_dimension=0,
        tiled=True,
    )
    kernel_part, gain_part = (
        lax.psum_scatter(kernel_term, "dp", scatter_dimension=0, tiled=True),
        lax.psum_scatter(gain_term, "dp", scatter_dimension=0, tiled=True),
    )
    proj_total, kernel_total, gain_total = lax.psum((proj_part, kernel_part, gain_part), "tm")
    grad_projection = proj_total.astype(jnp.bfloat16)
    return (
        grad_queries,
        grad_keys,
        grad_values,
        grad_projection,
        grad_glu,
        kernel_total,
        gain_total,
    )


def solution(mesh):
    in_specs = (
        P("dp", "tm", None),
        P("dp", "tm", None),
        P("dp", "tm", None),
        P("dp"),
        P("dp", None),
        P("dp", "tm", None),
        P("dp", "tm", None),
        P("dp", None),
        P("dp"),
        P("dp", "tm", None),
    )
    out_specs = (
        P("dp", "tm", None),
        P("dp", "tm", None),
        P("dp", "tm", None),
        P("dp", None),
        P("dp", "tm", None),
        P("dp", None),
        P("dp"),
    )
    return jax.shard_map(
        per_device, mesh=mesh, in_specs=in_specs, out_specs=out_specs, check_vma=False
    )
```

profile of v0, /device:TPU:4, one launch (start us, length us, event | category | flops | bytes accessed | tf_op | source)
XLA Modules:
  0.0 809.6 jit_solution(5044786274540221472)
XLA Ops:
  8.1 3.0 fusion.18
  12.9 3.1 collective-permute-start.8
  17.3 41.1 %all-gather = bf16[32,64,31]{1,2,0:T(8,128)(2,1)S(1)} all-gather(bf16[1,64,31]{1,2,0:T(8,128)(2,1)S(1)} %bitcast.320), channel_id=1, replica_groups=mesh['dp'=32,'tm'=8] {'dp'}, dimensions={0}, use_global_device_ids=true | all-gather | bytes 130944 | tf_op jit(solution)/shard_map/all_gather | solution.py:107
  64.8 64.7 %all-reduce = bf16[2048]{0:T(1024)(128)(2,1)S(1)} all-reduce(bf16[2048]{0:T(1024)(128)(2,1)S(1)} %dynamic-update-slice), channel_id=1, replica_groups=mesh['dp'=32,'tm'=8] {'dp'}, use_global_device_ids=true, to_apply=%add | all-reduce | flops 2048 | bytes 8192
  129.6 43.8 %fusion.190 = (f32[384]{0:T(512)S(1)}, f32[384,2048]{1,0:T(8,128)S(1)}) fusion(f32[2048]{0:T(1024)S(1)} %bitcast.229, bf16[15,2048]{1,0:T(8,128)(2,1)S(1)} %collective-permute-done.9, bf16[384,2048]{1,0:T(8,128)(2,1)} %copy-done.3, f32[2048]{0:T(1024)} %bitcast.231, f32[2048]{0:T(1024)} %bitcast.233, f32[2048]{0:T(1024)} %bitcast.235, f32[2048]{0:T(1024)} %bitcast.237, ...), kind=kLoop, calls=%fused_computation.373 | loop fusion | flops 143916672 | bytes 5096960 | tf_op jit(solution)/shard_map/reduce_sum | solution.py:69
  173.9 3.1 multiply_reduce_fusion
  177.1 12.4 %fusion.98 = (f32[2048]{0:T(1024)}, f32[2048]{0:T(1024)}, f32[2048]{0:T(1024)}, f32[2048]{0:T(1024)}, f32[2048]{0:T(1024)}, /*index=5*/f32[2048]{0:T(1024)}, f32...) fusion(bf16[15,2048]{1,0:T(8,128)(2,1)S(1)} %collective-permute-done.9, ...), kind=kLoop, calls=%fused_computation.234 | loop fusion | flops 49526784 | bytes 9586688 | tf_op jit(solution)/shard_map/reduce_sum | solution.py:61
  189.4 7.3 fusion.97
  196.8 4.7 fusion.82
  201.5 3.6 fusion.81
  205.1 3.5 stack.127
  210.7 9.6 %reduce-scatter.5.cloned.1.call-start = ((), (), s32[]{:S(2)}) async-start(), calls=%async_computation.3 | async-start | bytes 4325376 | tf_op jit(solution)/shard_map/reduce_scatter | solution.py:232
  232.3 88.0 %while.48 = (s32[]{:T(128)}, bf16[384,2,128]{2,0,1:T(8,128)(2,1)}, bf16[384,2,128]{2,0,1:T(8,128)(2,1)}, f32[2,384]{1,0:T(2,128)S(1)}, f32[2,384]{1,0:T(2,128)S(...) while((s32[]{:T(128)}, bf16[384,2,128]{2,0,1:T(8,128)(2,1)}, ...), condition=%wide.region_3.4_spmd.clone, body=%wide.region_0.3_spmd.clone.sunk | while | flops 530552064 | bytes 12043402 | solution.py:151
  233.2 2.6 collective-permute-start
  237.5 2.9 collective-permute-start.1
  242.6 3.2 fusion.255
  249.8 3.0 collective-permute-start.1
  255.1 3.3 fusion.255
  266.7 3.3 fusion.255
  270.0 3.3 collective-permute-done
  280.3 3.3 fusion.255
  291.8 3.3 fusion.255
  303.0 3.3 fusion.255
  306.6 2.8 collective-permute-done.1
  315.2 3.3 fusion.255
  325.9 5.2 collective-permute-start.11
  334.3 67.0 %all-reduce.1 = f32[2048]{0:T(1024)} all-reduce(f32[2048]{0:T(1024)} %get-tuple-element.705), channel_id=4, replica_groups=mesh['dp'=32,'tm'=8] {'dp'}, use_global_device_ids=true, to_apply=%region_48.49.clone | all-reduce | flops 2048 | bytes 16384
  402.9 46.6 %fusion.104 = (bf16[1,384,2048]{2,1,0:T(8,128)(2,1)S(1)}, f32[384,2048]{1,0:T(8,128)S(1)}) fusion(bf16[384,4096]{1,0:T(8,128)(2,1)} %bitcast.213, f32[384]{0:T(512)S(1)} %copy-done.50, f32[2048]{0:T(1024)S(1)} %bitcast.230, bf16[384,2048]{1,0:T(8,128)(2,1)} %copy-done.5, bf16[15,2048]{1,0:T(8,128)(2,1)} %collective-permute-done.11, f32[2048]{0:T(1024)S(1)} %bitcast.232, ...), kind=kLoop, calls=%fused_computation.250 | loop fusion | flops 148635648 | bytes 8242688 | tf_op jit(solution)/shard_map/concatenate | solution.py:230
  454.2 3.0 fusion.174
  459.1 3.2 convolution_bitcast_fusion.4
  465.0 277.5 %while.49 = (s32[]{:T(128)}, bf16[384,2,128]{2,0,1:T(8,128)(2,1)}, bf16[384,2,128]{2,0,1:T(8,128)(2,1)}, f32[384,2,128]{2,0,1:T(8,128)}, f32[384,2,128]{2,0,1:T(...) while((s32[]{:T(128)}, bf16[384,2,128]{2,0,1:T(8,128)(2,1)}, ...), condition=%wide.region_7.8_spmd.clone, body=%wide.region_6.7_spmd.clone.sunk | while | flops 380240640 | bytes 16915696 | solution.py:200
  482.9 18.6 %collective-permute-done.2 = bf16[384,2,128]{2,0,1:T(8,128)(2,1)} collective-permute-done((bf16[384,2,128]{2,0,1:T(8,128)(2,1)}, bf16[384,2,128]{2,0,1:T(8,128)(2,1)}, u32[]{:S(2)}, u32[]{:S(2)}) %collective-permute-start.2) | collective-permute-done | bytes 196640 | tf_op jit(solution)/shard_map/while/body/eval_jaxpr/ppermute | solution.py:19
  501.5 3.1 collective-permute-done.3
  516.2 2.7 collective-permute-start.3
  518.9 2.3 fusion.270
  521.2 29.3 %collective-permute-done.2 = bf16[384,2,128]{2,0,1:T(8,128)(2,1)} collective-permute-done((bf16[384,2,128]{2,0,1:T(8,128)(2,1)}, bf16[384,2,128]{2,0,1:T(8,128)(2,1)}, u32[]{:S(2)}, u32[]{:S(2)}) %collective-permute-start.2) | collective-permute-done | bytes 196640 | tf_op jit(solution)/shard_map/while/body/eval_jaxpr/ppermute | solution.py:19
  550.5 3.5 collective-permute-done.3
  569.8 22.1 %collective-permute-done.2 = bf16[384,2,128]{2,0,1:T(8,128)(2,1)} collective-permute-done((bf16[384,2,128]{2,0,1:T(8,128)(2,1)}, bf16[384,2,128]{2,0,1:T(8,128)(2,1)}, u32[]{:S(2)}, u32[]{:S(2)}) %collective-permute-start.2) | collective-permute-done | bytes 196640 | tf_op jit(solution)/shard_map/while/body/eval_jaxpr/ppermute | solution.py:19
  591.9 2.6 collective-permute-done.3
  608.4 22.2 %collective-permute-done.2 = bf16[384,2,128]{2,0,1:T(8,128)(2,1)} collective-permute-done((bf16[384,2,128]{2,0,1:T(8,128)(2,1)}, bf16[384,2,128]{2,0,1:T(8,128)(2,1)}, u32[]{:S(2)}, u32[]{:S(2)}) %collective-permute-start.2) | collective-permute-done | bytes 196640 | tf_op jit(solution)/shard_map/while/body/eval_jaxpr/ppermute | solution.py:19
  644.4 2.3 fusion.270
  646.7 21.4 %collective-permute-done.2 = bf16[384,2,128]{2,0,1:T(8,128)(2,1)} collective-permute-done((bf16[384,2,128]{2,0,1:T(8,128)(2,1)}, bf16[384,2,128]{2,0,1:T(8,128)(2,1)}, u32[]{:S(2)}, u32[]{:S(2)}) %collective-permute-start.2) | collective-permute-done | bytes 196640 | tf_op jit(solution)/shard_map/while/body/eval_jaxpr/ppermute | solution.py:19
  684.1 20.5 %collective-permute-done.2 = bf16[384,2,128]{2,0,1:T(8,128)(2,1)} collective-permute-done((bf16[384,2,128]{2,0,1:T(8,128)(2,1)}, bf16[384,2,128]{2,0,1:T(8,128)(2,1)}, u32[]{:S(2)}, u32[]{:S(2)}) %collective-permute-start.2) | collective-permute-done | bytes 196640 | tf_op jit(solution)/shard_map/while/body/eval_jaxpr/ppermute | solution.py:19
  720.7 19.7 %collective-permute-done.2 = bf16[384,2,128]{2,0,1:T(8,128)(2,1)} collective-permute-done((bf16[384,2,128]{2,0,1:T(8,128)(2,1)}, bf16[384,2,128]{2,0,1:T(8,128)(2,1)}, u32[]{:S(2)}, u32[]{:S(2)}) %collective-permute-start.2) | collective-permute-done | bytes 196640 | tf_op jit(solution)/shard_map/while/body/eval_jaxpr/ppermute | solution.py:19
  742.5 2.4 convolution_multiply_fusion.2
  744.9 2.6 copy.127
  749.5 2.6 fusion.171
  766.4 35.7 %all-reduce.4 = (bf16[128,256]{0,1:T(8,128)(2,1)S(1)}, f32[64,31]{0,1:T(8,128)}, f32[64]{0:T(128)}) all-reduce(f32[128,256]{0,1:T(8,128)} %reduce-scatter.5.cloned.1.call-done, f32[64,31]{0,1:T(8,128)S(1)} %copy-done.42, f32[64]{0:T(128)} %dynamic-slice.2), channel_id=1, replica_groups=mesh['dp'=32,'tm'=8] {'tm'}, use_global_device_ids=true, to_apply=%region_9.10 | all-reduce | flops 34816 | bytes 212992 | tf_op jit(solution)/shard_map/psum | solution.py:247
  (384 shorter events, 215.6 us)
Async XLA Ops:
  7.2 445.5 %reduce-scatter.7.cloned.1.call-start = ((), (), s32[]{:S(2)}) async-start(), calls=%async_computation.4 | async-start | bytes 1081344
  12.9 116.7 %collective-permute-start.8 = (bf16[15,2048]{1,0:T(8,128)(2,1)}, bf16[15,2048]{1,0:T(8,128)(2,1)S(1)}, u32[]{:S(2)}, u32[]{:S(2)}) collective-permute-start(bf16[15,2048]{1,0:T(8,128)(2,1)} %get-tuple-element.798), channel_id=1, source_target_pairs={{0,1},{1,2},{2,3},{3,4},{4,5},{5,6},{6,7},{8,9},{9,10},{10,11},{11... | collective-permute-start | bytes 184328 | tf_op jit(solution)/shard_map/ppermute | solution.py:30
  16.0 113.6 %collective-permute-start.9 = (bf16[15,2048]{1,0:T(8,128)(2,1)}, bf16[15,2048]{1,0:T(8,128)(2,1)S(1)}, u32[]{:S(2)}, u32[]{:S(2)}) collective-permute-start(bf16[15,2048]{1,0:T(8,128)(2,1)} %get-tuple-element.799), channel_id=1, source_target_pairs={{1,0},{2,1},{3,2},{4,3},{5,4},{6,5},{7,6},{9,8},{10,9},{11,10},{12... | collective-permute-start | bytes 184328 | tf_op jit(solution)/shard_map/ppermute | solution.py:32
  209.9 244.2 %all-gather.3.cloned.1.call-start = ((), (), s32[]{:S(2)}) async-start(), calls=%async_computation.2 | async-start | bytes 2162688 | tf_op jit(solution)/shard_map/all_gather | solution.py:106
  210.7 555.7 %reduce-scatter.5.cloned.1.call-start = ((), (), s32[]{:S(2)}) async-start(), calls=%async_computation.3 | async-start | bytes 4325376 | tf_op jit(solution)/shard_map/reduce_scatter | solution.py:232
  233.2 12.6 %collective-permute-start = (bf16[384,2,128]{2,0,1:T(8,128)(2,1)S(1)}, bf16[384,2,128]{2,0,1:T(8,128)(2,1)}, u32[]{:S(2)}, u32[]{:S(2)}) collective-permute-start(bf16[384,2,128]{2,0,1:T(8,128)(2,1)S(1)} %copy.173), channel_id=1, source_target_pairs={{7,0},{0,1},{1,2},{2,3},{3,4},{4,5},{5,6},{6,7},{15,8},{8,9},{9,10... | collective-permute-start | bytes 589832 | tf_op jit(solution)/shard_map/while/body/eval_jaxpr/ppermute | solution.py:19
  237.5 9.7 %collective-permute-start.1 = (bf16[384,2,128]{2,0,1:T(8,128)(2,1)}, bf16[384,2,128]{2,0,1:T(8,128)(2,1)}, u32[]{:S(2)}, u32[]{:S(2)}) collective-permute-start(bf16[384,2,128]{2,0,1:T(8,128)(2,1)} %copy.174), channel_id=1, source_target_pairs={{7,0},{0,1},{1,2},{2,3},{3,4},{4,5},{5,6},{6,7},{15,8},{8,9},{9,10... | collective-permute-start | bytes 589832 | tf_op jit(solution)/shard_map/while/body/eval_jaxpr/ppermute | solution.py:19
  248.1 10.3 %collective-permute-start = (bf16[384,2,128]{2,0,1:T(8,128)(2,1)S(1)}, bf16[384,2,128]{2,0,1:T(8,128)(2,1)}, u32[]{:S(2)}, u32[]{:S(2)}) collective-permute-start(bf16[384,2,128]{2,0,1:T(8,128)(2,1)S(1)} %copy.173), channel_id=1, source_target_pairs={{7,0},{0,1},{1,2},{2,3},{3,4},{4,5},{5,6},{6,7},{15,8},{8,9},{9,10... | collective-permute-start | bytes 589832 | tf_op jit(solution)/shard_map/while/body/eval_jaxpr/ppermute | solution.py:19
  249.8 10.6 %collective-permute-start.1 = (bf16[384,2,128]{2,0,1:T(8,128)(2,1)}, bf16[384,2,128]{2,0,1:T(8,128)(2,1)}, u32[]{:S(2)}, u32[]{:S(2)}) collective-permute-start(bf16[384,2,128]{2,0,1:T(8,128)(2,1)} %copy.174), channel_id=1, source_target_pairs={{7,0},{0,1},{1,2},{2,3},{3,4},{4,5},{5,6},{6,7},{15,8},{8,9},{9,10... | collective-permute-start | bytes 589832 | tf_op jit(solution)/shard_map/while/body/eval_jaxpr/ppermute | solution.py:19
  261.3 12.0 %collective-permute-start = (bf16[384,2,128]{2,0,1:T(8,128)(2,1)S(1)}, bf16[384,2,128]{2,0,1:T(8,128)(2,1)}, u32[]{:S(2)}, u32[]{:S(2)}) collective-permute-start(bf16[384,2,128]{2,0,1:T(8,128)(2,1)S(1)} %copy.173), channel_id=1, source_target_pairs={{7,0},{0,1},{1,2},{2,3},{3,4},{4,5},{5,6},{6,7},{15,8},{8,9},{9,10... | collective-permute-start | bytes 589832 | tf_op jit(solution)/shard_map/while/body/eval_jaxpr/ppermute | solution.py:19
  262.9 12.5 %collective-permute-start.1 = (bf16[384,2,128]{2,0,1:T(8,128)(2,1)}, bf16[384,2,128]{2,0,1:T(8,128)(2,1)}, u32[]{:S(2)}, u32[]{:S(2)}) collective-permute-start(bf16[384,2,128]{2,0,1:T(8,128)(2,1)} %copy.174), channel_id=1, source_target_pairs={{7,0},{0,1},{1,2},{2,3},{3,4},{4,5},{5,6},{6,7},{15,8},{8,9},{9,10... | collective-permute-start | bytes 589832 | tf_op jit(solution)/shard_map/while/body/eval_jaxpr/ppermute | solution.py:19
  276.3 8.4 %collective-permute-start = (bf16[384,2,128]{2,0,1:T(8,128)(2,1)S(1)}, bf16[384,2,128]{2,0,1:T(8,128)(2,1)}, u32[]{:S(2)}, u32[]{:S(2)}) collective-permute-start(bf16[384,2,128]{2,0,1:T(8,128)(2,1)S(1)} %copy.173), channel_id=1, source_target_pairs={{7,0},{0,1},{1,2},{2,3},{3,4},{4,5},{5,6},{6,7},{15,8},{8,9},{9,10... | collective-permute-start | bytes 589832 | tf_op jit(solution)/shard_map/while/body/eval_jaxpr/ppermute | solution.py:19
  277.9 8.9 %collective-permute-start.1 = (bf16[384,2,128]{2,0,1:T(8,128)(2,1)}, bf16[384,2,128]{2,0,1:T(8,128)(2,1)}, u32[]{:S(2)}, u32[]{:S(2)}) collective-permute-start(bf16[384,2,128]{2,0,1:T(8,128)(2,1)} %copy.174), channel_id=1, source_target_pairs={{7,0},{0,1},{1,2},{2,3},{3,4},{4,5},{5,6},{6,7},{15,8},{8,9},{9,10... | collective-permute-start | bytes 589832 | tf_op jit(solution)/shard_map/while/body/eval_jaxpr/ppermute | solution.py:19
  289.4 8.4 %collective-permute-start.1 = (bf16[384,2,128]{2,0,1:T(8,128)(2,1)}, bf16[384,2,128]{2,0,1:T(8,128)(2,1)}, u32[]{:S(2)}, u32[]{:S(2)}) collective-permute-start(bf16[384,2,128]{2,0,1:T(8,128)(2,1)} %copy.174), channel_id=1, source_target_pairs={{7,0},{0,1},{1,2},{2,3},{3,4},{4,5},{5,6},{6,7},{15,8},{8,9},{9,10... | collective-permute-start | bytes 589832 | tf_op jit(solution)/shard_map/while/body/eval_jaxpr/ppermute | solution.py:19
  300.3 9.1 %collective-permute-start.1 = (bf16[384,2,128]{2,0,1:T(8,128)(2,1)}, bf16[384,2,128]{2,0,1:T(8,128)(2,1)}, u32[]{:S(2)}, u32[]{:S(2)}) collective-permute-start(bf16[384,2,128]{2,0,1:T(8,128)(2,1)} %copy.174), channel_id=1, source_target_pairs={{7,0},{0,1},{1,2},{2,3},{3,4},{4,5},{5,6},{6,7},{15,8},{8,9},{9,10... | collective-permute-start | bytes 589832 | tf_op jit(solution)/shard_map/while/body/eval_jaxpr/ppermute | solution.py:19
  310.3 8.2 %collective-permute-start = (bf16[384,2,128]{2,0,1:T(8,128)(2,1)S(1)}, bf16[384,2,128]{2,0,1:T(8,128)(2,1)}, u32[]{:S(2)}, u32[]{:S(2)}) collective-permute-start(bf16[384,2,128]{2,0,1:T(8,128)(2,1)S(1)} %copy.173), channel_id=1, source_target_pairs={{7,0},{0,1},{1,2},{2,3},{3,4},{4,5},{5,6},{6,7},{15,8},{8,9},{9,10... | collective-permute-start | bytes 589832 | tf_op jit(solution)/shard_map/while/body/eval_jaxpr/ppermute | solution.py:19
  311.9 8.4 %collective-permute-start.1 = (bf16[384,2,128]{2,0,1:T(8,128)(2,1)}, bf16[384,2,128]{2,0,1:T(8,128)(2,1)}, u32[]{:S(2)}, u32[]{:S(2)}) collective-permute-start(bf16[384,2,128]{2,0,1:T(8,128)(2,1)} %copy.174), channel_id=1, source_target_pairs={{7,0},{0,1},{1,2},{2,3},{3,4},{4,5},{5,6},{6,7},{15,8},{8,9},{9,10... | collective-permute-start | bytes 589832 | tf_op jit(solution)/shard_map/while/body/eval_jaxpr/ppermute | solution.py:19
  324.7 78.0 %collective-permute-start.10 = (bf16[15,2048]{1,0:T(8,128)(2,1)}, bf16[15,2048]{1,0:T(8,128)(2,1)}, u32[]{:S(2)}, u32[]{:S(2)}) collective-permute-start(bf16[15,2048]{1,0:T(8,128)(2,1)} %get-tuple-element.796), channel_id=1, source_target_pairs={{1,0},{2,1},{3,2},{4,3},{5,4},{6,5},{7,6},{9,8},{10,9},{11,10},{12... | collective-permute-start | bytes 184328 | tf_op jit(solution)/shard_map/ppermute | solution.py:32
  325.9 76.7 %collective-permute-start.11 = (bf16[15,2048]{1,0:T(8,128)(2,1)}, bf16[15,2048]{1,0:T(8,128)(2,1)}, u32[]{:S(2)}, u32[]{:S(2)}) collective-permute-start(bf16[15,2048]{1,0:T(8,128)(2,1)} %get-tuple-element.797), channel_id=1, source_target_pairs={{0,1},{1,2},{2,3},{3,4},{4,5},{5,6},{6,7},{8,9},{9,10},{10,11},{11... | collective-permute-start | bytes 184328 | tf_op jit(solution)/shard_map/ppermute | solution.py:30
  474.5 30.1 %collective-permute-start.4 = (f32[384,2,128]{2,0,1:T(8,128)}, f32[384,2,128]{2,0,1:T(8,128)}, u32[]{:S(2)}, u32[]{:S(2)}) collective-permute-start(f32[384,2,128]{2,0,1:T(8,128)} %fusion.268), channel_id=1, source_target_pairs={{7,0},{0,1},{1,2},{2,3},{3,4},{4,5},{5,6},{6,7},{15,8},{8,9},{9,10... | collective-permute-start | bytes 1179656 | tf_op jit(solution)/shard_map/while/body/eval_jaxpr/ppermute | solution.py:19
  476.6 28.0 %collective-permute-start.5 = (f32[384,2,128]{2,0,1:T(8,128)}, f32[384,2,128]{2,0,1:T(8,128)}, u32[]{:S(2)}, u32[]{:S(2)}) collective-permute-start(f32[384,2,128]{2,0,1:T(8,128)} %fusion.269), channel_id=1, source_target_pairs={{7,0},{0,1},{1,2},{2,3},{3,4},{4,5},{5,6},{6,7},{15,8},{8,9},{9,10... | collective-permute-start | bytes 1179656 | tf_op jit(solution)/shard_map/while/body/eval_jaxpr/ppermute | solution.py:19
  477.0 24.5 %collective-permute-start.2 = (bf16[384,2,128]{2,0,1:T(8,128)(2,1)}, bf16[384,2,128]{2,0,1:T(8,128)(2,1)}, u32[]{:S(2)}, u32[]{:S(2)}) collective-permute-start(bf16[384,2,128]{2,0,1:T(8,128)(2,1)} %copy.191), channel_id=1, source_target_pairs={{7,0},{0,1},{1,2},{2,3},{3,4},{4,5},{5,6},{6,7},{15,8},{8,9},{9,10... | collective-permute-start | bytes 589832 | tf_op jit(solution)/shard_map/while/body/eval_jaxpr/ppermute | solution.py:19
  479.0 25.6 %collective-permute-start.3 = (bf16[384,2,128]{2,0,1:T(8,128)(2,1)}, bf16[384,2,128]{2,0,1:T(8,128)(2,1)}, u32[]{:S(2)}, u32[]{:S(2)}) collective-permute-start(bf16[384,2,128]{2,0,1:T(8,128)(2,1)} %copy.192), channel_id=1, source_target_pairs={{7,0},{0,1},{1,2},{2,3},{3,4},{4,5},{5,6},{6,7},{15,8},{8,9},{9,10... | collective-permute-start | bytes 589832 | tf_op jit(solution)/shard_map/while/body/eval_jaxpr/ppermute | solution.py:19
  514.1 39.9 %collective-permute-start.4 = (f32[384,2,128]{2,0,1:T(8,128)}, f32[384,2,128]{2,0,1:T(8,128)}, u32[]{:S(2)}, u32[]{:S(2)}) collective-permute-start(f32[384,2,128]{2,0,1:T(8,128)} %fusion.268), channel_id=1, source_target_pairs={{7,0},{0,1},{1,2},{2,3},{3,4},{4,5},{5,6},{6,7},{15,8},{8,9},{9,10... | collective-permute-start | bytes 1179656 | tf_op jit(solution)/shard_map/while/body/eval_jaxpr/ppermute | solution.py:19
  516.2 37.8 %collective-permute-start.5 = (f32[384,2,128]{2,0,1:T(8,128)}, f32[384,2,128]{2,0,1:T(8,128)}, u32[]{:S(2)}, u32[]{:S(2)}) collective-permute-start(f32[384,2,128]{2,0,1:T(8,128)} %fusion.269), channel_id=1, source_target_pairs={{7,0},{0,1},{1,2},{2,3},{3,4},{4,5},{5,6},{6,7},{15,8},{8,9},{9,10... | collective-permute-start | bytes 1179656 | tf_op jit(solution)/shard_map/while/body/eval_jaxpr/ppermute | solution.py:19
  516.2 34.3 %collective-permute-start.2 = (bf16[384,2,128]{2,0,1:T(8,128)(2,1)}, bf16[384,2,128]{2,0,1:T(8,128)(2,1)}, u32[]{:S(2)}, u32[]{:S(2)}) collective-permute-start(bf16[384,2,128]{2,0,1:T(8,128)(2,1)} %copy.191), channel_id=1, source_target_pairs={{7,0},{0,1},{1,2},{2,3},{3,4},{4,5},{5,6},{6,7},{15,8},{8,9},{9,10... | collective-permute-start | bytes 589832 | tf_op jit(solution)/shard_map/while/body/eval_jaxpr/ppermute | solution.py:19
  516.2 37.8 %collective-permute-start.3 = (bf16[384,2,128]{2,0,1:T(8,128)(2,1)}, bf16[384,2,128]{2,0,1:T(8,128)(2,1)}, u32[]{:S(2)}, u32[]{:S(2)}) collective-permute-start(bf16[384,2,128]{2,0,1:T(8,128)(2,1)} %copy.192), channel_id=1, source_target_pairs={{7,0},{0,1},{1,2},{2,3},{3,4},{4,5},{5,6},{6,7},{15,8},{8,9},{9,10... | collective-permute-start | bytes 589832 | tf_op jit(solution)/shard_map/while/body/eval_jaxpr/ppermute | solution.py:19
  563.5 31.1 %collective-permute-start.4 = (f32[384,2,128]{2,0,1:T(8,128)}, f32[384,2,128]{2,0,1:T(8,128)}, u32[]{:S(2)}, u32[]{:S(2)}) collective-permute-start(f32[384,2,128]{2,0,1:T(8,128)} %fusion.268), channel_id=1, source_target_pairs={{7,0},{0,1},{1,2},{2,3},{3,4},{4,5},{5,6},{6,7},{15,8},{8,9},{9,10... | collective-permute-start | bytes 1179656 | tf_op jit(solution)/shard_map/while/body/eval_jaxpr/ppermute | solution.py:19
  565.6 28.9 %collective-permute-start.5 = (f32[384,2,128]{2,0,1:T(8,128)}, f32[384,2,128]{2,0,1:T(8,128)}, u32[]{:S(2)}, u32[]{:S(2)}) collective-permute-start(f32[384,2,128]{2,0,1:T(8,128)} %fusion.269), channel_id=1, source_target_pairs={{7,0},{0,1},{1,2},{2,3},{3,4},{4,5},{5,6},{6,7},{15,8},{8,9},{9,10... | collective-permute-start | bytes 1179656 | tf_op jit(solution)/shard_map/while/body/eval_jaxpr/ppermute | solution.py:19
  565.6 26.3 %collective-permute-start.2 = (bf16[384,2,128]{2,0,1:T(8,128)(2,1)}, bf16[384,2,128]{2,0,1:T(8,128)(2,1)}, u32[]{:S(2)}, u32[]{:S(2)}) collective-permute-start(bf16[384,2,128]{2,0,1:T(8,128)(2,1)} %copy.191), channel_id=1, source_target_pairs={{7,0},{0,1},{1,2},{2,3},{3,4},{4,5},{5,6},{6,7},{15,8},{8,9},{9,10... | collective-permute-start | bytes 589832 | tf_op jit(solution)/shard_map/while/body/eval_jaxpr/ppermute | solution.py:19
  565.6 28.9 %collective-permute-start.3 = (bf16[384,2,128]{2,0,1:T(8,128)(2,1)}, bf16[384,2,128]{2,0,1:T(8,128)(2,1)}, u32[]{:S(2)}, u32[]{:S(2)}) collective-permute-start(bf16[384,2,128]{2,0,1:T(8,128)(2,1)} %copy.192), channel_id=1, source_target_pairs={{7,0},{0,1},{1,2},{2,3},{3,4},{4,5},{5,6},{6,7},{15,8},{8,9},{9,10... | collective-permute-start | bytes 589832 | tf_op jit(solution)/shard_map/while/body/eval_jaxpr/ppermute | solution.py:19
  604.0 28.8 %collective-permute-start.4 = (f32[384,2,128]{2,0,1:T(8,128)}, f32[384,2,128]{2,0,1:T(8,128)}, u32[]{:S(2)}, u32[]{:S(2)}) collective-permute-start(f32[384,2,128]{2,0,1:T(8,128)} %fusion.268), channel_id=1, source_target_pairs={{7,0},{0,1},{1,2},{2,3},{3,4},{4,5},{5,6},{6,7},{15,8},{8,9},{9,10... | collective-permute-start | bytes 1179656 | tf_op jit(solution)/shard_map/while/body/eval_jaxpr/ppermute | solution.py:19
  606.1 26.7 %collective-permute-start.5 = (f32[384,2,128]{2,0,1:T(8,128)}, f32[384,2,128]{2,0,1:T(8,128)}, u32[]{:S(2)}, u32[]{:S(2)}) collective-permute-start(f32[384,2,128]{2,0,1:T(8,128)} %fusion.269), channel_id=1, source_target_pairs={{7,0},{0,1},{1,2},{2,3},{3,4},{4,5},{5,6},{6,7},{15,8},{8,9},{9,10... | collective-permute-start | bytes 1179656 | tf_op jit(solution)/shard_map/while/body/eval_jaxpr/ppermute | solution.py:19
  606.1 24.6 %collective-permute-start.2 = (bf16[384,2,128]{2,0,1:T(8,128)(2,1)}, bf16[384,2,128]{2,0,1:T(8,128)(2,1)}, u32[]{:S(2)}, u32[]{:S(2)}) collective-permute-start(bf16[384,2,128]{2,0,1:T(8,128)(2,1)} %copy.191), channel_id=1, source_target_pairs={{7,0},{0,1},{1,2},{2,3},{3,4},{4,5},{5,6},{6,7},{15,8},{8,9},{9,10... | collective-permute-start | bytes 589832 | tf_op jit(solution)/shard_map/while/body/eval_jaxpr/ppermute | solution.py:19
  606.1 26.7 %collective-permute-start.3 = (bf16[384,2,128]{2,0,1:T(8,128)(2,1)}, bf16[384,2,128]{2,0,1:T(8,128)(2,1)}, u32[]{:S(2)}, u32[]{:S(2)}) collective-permute-start(bf16[384,2,128]{2,0,1:T(8,128)(2,1)} %copy.192), channel_id=1, source_target_pairs={{7,0},{0,1},{1,2},{2,3},{3,4},{4,5},{5,6},{6,7},{15,8},{8,9},{9,10... | collective-permute-start | bytes 589832 | tf_op jit(solution)/shard_map/while/body/eval_jaxpr/ppermute | solution.py:19
  642.3 27.9 %collective-permute-start.4 = (f32[384,2,128]{2,0,1:T(8,128)}, f32[384,2,128]{2,0,1:T(8,128)}, u32[]{:S(2)}, u32[]{:S(2)}) collective-permute-start(f32[384,2,128]{2,0,1:T(8,128)} %fusion.268), channel_id=1, source_target_pairs={{7,0},{0,1},{1,2},{2,3},{3,4},{4,5},{5,6},{6,7},{15,8},{8,9},{9,10... | collective-permute-start | bytes 1179656 | tf_op jit(solution)/shard_map/while/body/eval_jaxpr/ppermute | solution.py:19
  644.4 25.8 %collective-permute-start.5 = (f32[384,2,128]{2,0,1:T(8,128)}, f32[384,2,128]{2,0,1:T(8,128)}, u32[]{:S(2)}, u32[]{:S(2)}) collective-permute-start(f32[384,2,128]{2,0,1:T(8,128)} %fusion.269), channel_id=1, source_target_pairs={{7,0},{0,1},{1,2},{2,3},{3,4},{4,5},{5,6},{6,7},{15,8},{8,9},{9,10... | collective-permute-start | bytes 1179656 | tf_op jit(solution)/shard_map/while/body/eval_jaxpr/ppermute | solution.py:19
  644.4 23.7 %collective-permute-start.2 = (bf16[384,2,128]{2,0,1:T(8,128)(2,1)}, bf16[384,2,128]{2,0,1:T(8,128)(2,1)}, u32[]{:S(2)}, u32[]{:S(2)}) collective-permute-start(bf16[384,2,128]{2,0,1:T(8,128)(2,1)} %copy.191), channel_id=1, source_target_pairs={{7,0},{0,1},{1,2},{2,3},{3,4},{4,5},{5,6},{6,7},{15,8},{8,9},{9,10... | collective-permute-start | bytes 589832 | tf_op jit(solution)/shard_map/while/body/eval_jaxpr/ppermute | solution.py:19
  644.4 25.8 %collective-permute-start.3 = (bf16[384,2,128]{2,0,1:T(8,128)(2,1)}, bf16[384,2,128]{2,0,1:T(8,128)(2,1)}, u32[]{:S(2)}, u32[]{:S(2)}) collective-permute-start(bf16[384,2,128]{2,0,1:T(8,128)(2,1)} %copy.192), channel_id=1, source_target_pairs={{7,0},{0,1},{1,2},{2,3},{3,4},{4,5},{5,6},{6,7},{15,8},{8,9},{9,10... | collective-permute-start | bytes 589832 | tf_op jit(solution)/shard_map/while/body/eval_jaxpr/ppermute | solution.py:19
  679.7 27.1 %collective-permute-start.4 = (f32[384,2,128]{2,0,1:T(8,128)}, f32[384,2,128]{2,0,1:T(8,128)}, u32[]{:S(2)}, u32[]{:S(2)}) collective-permute-start(f32[384,2,128]{2,0,1:T(8,128)} %fusion.268), channel_id=1, source_target_pairs={{7,0},{0,1},{1,2},{2,3},{3,4},{4,5},{5,6},{6,7},{15,8},{8,9},{9,10... | collective-permute-start | bytes 1179656 | tf_op jit(solution)/shard_map/while/body/eval_jaxpr/ppermute | solution.py:19
  681.8 25.0 %collective-permute-start.5 = (f32[384,2,128]{2,0,1:T(8,128)}, f32[384,2,128]{2,0,1:T(8,128)}, u32[]{:S(2)}, u32[]{:S(2)}) collective-permute-start(f32[384,2,128]{2,0,1:T(8,128)} %fusion.269), channel_id=1, source_target_pairs={{7,0},{0,1},{1,2},{2,3},{3,4},{4,5},{5,6},{6,7},{15,8},{8,9},{9,10... | collective-permute-start | bytes 1179656 | tf_op jit(solution)/shard_map/while/body/eval_jaxpr/ppermute | solution.py:19
  681.8 22.9 %collective-permute-start.2 = (bf16[384,2,128]{2,0,1:T(8,128)(2,1)}, bf16[384,2,128]{2,0,1:T(8,128)(2,1)}, u32[]{:S(2)}, u32[]{:S(2)}) collective-permute-start(bf16[384,2,128]{2,0,1:T(8,128)(2,1)} %copy.191), channel_id=1, source_target_pairs={{7,0},{0,1},{1,2},{2,3},{3,4},{4,5},{5,6},{6,7},{15,8},{8,9},{9,10... | collective-permute-start | bytes 589832 | tf_op jit(solution)/shard_map/while/body/eval_jaxpr/ppermute | solution.py:19
  681.8 25.0 %collective-permute-start.3 = (bf16[384,2,128]{2,0,1:T(8,128)(2,1)}, bf16[384,2,128]{2,0,1:T(8,128)(2,1)}, u32[]{:S(2)}, u32[]{:S(2)}) collective-permute-start(bf16[384,2,128]{2,0,1:T(8,128)(2,1)} %copy.192), channel_id=1, source_target_pairs={{7,0},{0,1},{1,2},{2,3},{3,4},{4,5},{5,6},{6,7},{15,8},{8,9},{9,10... | collective-permute-start | bytes 589832 | tf_op jit(solution)/shard_map/while/body/eval_jaxpr/ppermute | solution.py:19
  716.2 26.2 %collective-permute-start.4 = (f32[384,2,128]{2,0,1:T(8,128)}, f32[384,2,128]{2,0,1:T(8,128)}, u32[]{:S(2)}, u32[]{:S(2)}) collective-permute-start(f32[384,2,128]{2,0,1:T(8,128)} %fusion.268), channel_id=1, source_target_pairs={{7,0},{0,1},{1,2},{2,3},{3,4},{4,5},{5,6},{6,7},{15,8},{8,9},{9,10... | collective-permute-start | bytes 1179656 | tf_op jit(solution)/shard_map/while/body/eval_jaxpr/ppermute | solution.py:19
  718.3 24.1 %collective-permute-start.5 = (f32[384,2,128]{2,0,1:T(8,128)}, f32[384,2,128]{2,0,1:T(8,128)}, u32[]{:S(2)}, u32[]{:S(2)}) collective-permute-start(f32[384,2,128]{2,0,1:T(8,128)} %fusion.269), channel_id=1, source_target_pairs={{7,0},{0,1},{1,2},{2,3},{3,4},{4,5},{5,6},{6,7},{15,8},{8,9},{9,10... | collective-permute-start | bytes 1179656 | tf_op jit(solution)/shard_map/while/body/eval_jaxpr/ppermute | solution.py:19
  718.3 22.0 %collective-permute-start.2 = (bf16[384,2,128]{2,0,1:T(8,128)(2,1)}, bf16[384,2,128]{2,0,1:T(8,128)(2,1)}, u32[]{:S(2)}, u32[]{:S(2)}) collective-permute-start(bf16[384,2,128]{2,0,1:T(8,128)(2,1)} %copy.191), channel_id=1, source_target_pairs={{7,0},{0,1},{1,2},{2,3},{3,4},{4,5},{5,6},{6,7},{15,8},{8,9},{9,10... | collective-permute-start | bytes 589832 | tf_op jit(solution)/shard_map/while/body/eval_jaxpr/ppermute | solution.py:19
  718.3 24.1 %collective-permute-start.3 = (bf16[384,2,128]{2,0,1:T(8,128)(2,1)}, bf16[384,2,128]{2,0,1:T(8,128)(2,1)}, u32[]{:S(2)}, u32[]{:S(2)}) collective-permute-start(bf16[384,2,128]{2,0,1:T(8,128)(2,1)} %copy.192), channel_id=1, source_target_pairs={{7,0},{0,1},{1,2},{2,3},{3,4},{4,5},{5,6},{6,7},{15,8},{8,9},{9,10... | collective-permute-start | bytes 589832 | tf_op jit(solution)/shard_map/while/body/eval_jaxpr/ppermute | solution.py:19
  752.2 8.5 %collective-permute-start.7 = (bf16[384,2,128]{0,2,1:T(8,128)(2,1)}, bf16[384,2,128]{0,2,1:T(8,128)(2,1)}, u32[]{:S(2)}, u32[]{:S(2)}) collective-permute-start(bf16[384,2,128]{0,2,1:T(8,128)(2,1)} %fusion.171), channel_id=1, source_target_pairs={{7,0},{0,1},{1,2},{2,3},{3,4},{4,5},{5,6},{6,7},{15,8},{8,9},{9,10... | collective-permute-start | bytes 589832 | tf_op jit(solution)/shard_map/ppermute | solution.py:19
  (71 other events, 3089.9 us)
Sparse Core Ops, SparseCore 0:
  210.1 120.7 reduce-scatter.6
  333.7 76.8 all-gather.2
  462.4 137.8 reduce-scatter.4
where the time goes:
time: 816 us; the launch traced here: 810 us
  blocking collectives  209 us (26%)
  waiting for transfers between devices  195 us (24%)
  other arithmetic  142 us (17%)
  matrix products  110 us (13%)
  local copies, waits for them, and re-layouts  96.7 us (12%)
  starting transfers between devices  40.9 us (5%)
  between operations  17 us (2%)
    ppermute x44, waiting for transfers between devices, from_behind(): return lax.ppermute(block, axis, route)  194 us
    unnamed x2, blocking collectives  132 us
    while x63, local copies, waits for them, and re-layouts  53.4 us
    concatenate x3, other arithmetic, per_device(): jnp.concatenate([first_half, second_half], axis=-1).astype(jnp.bfloat16)  49.8 us
    reduce_sum x1, other arithmetic, norm_backward(): centre = mixed - jnp.mean(mixed, axis=-1, keepdims=True)  43.8 us
    all_gather x1, blocking collectives, per_device(): lax.all_gather(kernel, 'dp', axis=0, tiled=True)  41.1 us
    psum x1, blocking collectives, per_device(): lax.psum((proj_part, kernel_part, gain_part), 'tm')  35.7 us
    reduce_sum x4, other arithmetic, tap_products(): jnp.sum(grad_f * padded[tap:tap + frame_rows].astype(jnp.float32), axis=0)  28 us
  transfers between devices with their start and end apart: 51, of which 27 were waited for; matrix products, arithmetic and copies ran while one was open for 30% of the time, Pallas kernels for 0%

commit v1 on v0

--- a/solution.py
+++ b/solution.py
@@ -82,6 +82,47 @@
         - standard * jnp.mean(scaled * standard, axis=-1, keepdims=True)
     )
     return (grad_conv.astype(jnp.bfloat16), gain_term)
+
+
+def gather_params(projection, kernel, norm_gain):
+    width = projection.shape[1]
+    tail = jnp.concatenate([kernel.reshape(-1), norm_gain.reshape(-1)])
+    tail_rows = -(-tail.shape[0] // width)
+    tail = jnp.pad(tail, (0, tail_rows * width - tail.shape[0])).reshape(tail_rows, width)
+    block = jnp.concatenate([projection, tail], axis=0)
+    full = lax.all_gather(block, "dp", axis=0, tiled=False)
+    count = full.shape[0]
+    proj_rows = projection.shape[0]
+    full_proj = full[:, :proj_rows].reshape(count * proj_rows, width)
+    flat_tail = full[:, proj_rows:].reshape(count, tail_rows * width)
+    kernel_size = kernel.shape[0] * kernel.shape[1]
+    full_kernel = flat_tail[:, :kernel_size].reshape(count * kernel.shape[0], kernel.shape[1])
+    full_gain = flat_tail[:, kernel_size : kernel_size + norm_gain.shape[0]].reshape(-1)
+    return full_proj, full_kernel, full_gain
+
+
+def reduce_grads(proj_term, kernel_term, gain_term):
+    count = lax.axis_size("dp")
+    width = proj_term.shape[1]
+    proj_blocks = proj_term.reshape(count, -1, width)
+    proj_rows = proj_blocks.shape[1]
+    kernel_blocks = kernel_term.reshape(count, -1)
+    gain_blocks = gain_term.reshape(count, -1)
+    tail = jnp.concatenate([kernel_blocks, gain_blocks], axis=1)
+    tail_cols = tail.shape[1]
+    tail_rows = -(-tail_cols // width)
+    tail = jnp.pad(tail, ((0, 0), (0, tail_rows * width - tail_cols))).reshape(
+        count, tail_rows, width
+    )
+    packed = jnp.concatenate([proj_blocks, tail], axis=1).reshape(-1, width)
+    part = lax.psum_scatter(packed, "dp", scatter_dimension=0, tiled=True)
+    total = lax.psum(part, "tm")
+    proj_total = total[:proj_rows]
+    flat_tail = total[proj_rows:].reshape(-1)
+    kernel_size = kernel_blocks.shape[1]
+    kernel_total = flat_tail[:kernel_size].reshape(-1, kernel_term.shape[1])
+    gain_total = flat_tail[kernel_size : kernel_size + gain_blocks.shape[1]]
+    return proj_total, kernel_total, gain_total
 
 
 def per_device(
@@ -102,11 +143,7 @@
     flat_width = queries.shape[2]
     score_scale = HDIM ** (-0.5)
     length = lengths[0]
-    full_proj, full_kernel, full_gain = (
-        lax.all_gather(projection, "dp", axis=0, tiled=True),
-        lax.all_gather(kernel, "dp", axis=0, tiled=True),
-        lax.all_gather(norm_gain, "dp", axis=0, tiled=True),
-    )
+    full_proj, full_kernel, full_gain = gather_params(projection, kernel, norm_gain)
     query_heads = queries[0].reshape(frame_rows, HEADS, HDIM)
     key_heads = key_input[0].reshape(frame_rows, HEADS, HDIM)
     value_heads = value_input[0].reshape(frame_rows, HEADS, HDIM)
@@ -229,22 +266,13 @@
     second_half = grad_activ * linear * gate_sig * (1.0 - gate_sig)
     grad_glu = jnp.concatenate([first_half, second_half], axis=-1).astype(jnp.bfloat16)[None]
     attended_flat = attended.reshape(frame_rows, flat_width)
-    proj_part = lax.psum_scatter(
-        lax.dot_general(
-            upstream_rows,
-            attended_flat,
-            (((0,), (0,)), ((), ())),
-            preferred_element_type=jnp.float32,
-        ),
-        "dp",
-        scatter_dimension=0,
-        tiled=True,
-    )
-    kernel_part, gain_part = (
-        lax.psum_scatter(kernel_term, "dp", scatter_dimension=0, tiled=True),
-        lax.psum_scatter(gain_term, "dp", scatter_dimension=0, tiled=True),
-    )
-    proj_total, kernel_total, gain_total = lax.psum((proj_part, kernel_part, gain_part), "tm")
+    proj_term = lax.dot_general(
+        upstream_rows,
+        attended_flat,
+        (((0,), (0,)), ((), ())),
+        preferred_element_type=jnp.float32,
+    )
+    proj_total, kernel_total, gain_total = reduce_grads(proj_term, kernel_term, gain_term)
     grad_projection = proj_total.astype(jnp.bfloat16)
     return (
         grad_queries,

time: 816 us -> 667 us (0.82)
  blocking collectives: 209 us -> 0 us
  waiting for transfers between devices: 195 us -> 248 us
  matrix products: 110 us -> 76.7 us
  local copies, waits for them, and re-layouts: 96.7 us -> 116 us
  starting transfers between devices: 40.9 us -> 54 us
    unnamed x2 -> x0, blocking collectives: 132 us -> none
    psum x0 -> x1, waiting for transfers between devices: none -> 68 us  [reduce_grads(): total = lax.psum(part, 'tm')]
    all_gather x1 -> x0, blocking collectives: 41.1 us -> none  [per_device(): lax.all_gather(kernel, 'dp', axis=0, tiled=True)]
    psum x1 -> x0, blocking collectives: 35.7 us -> none  [per_device(): lax.psum((proj_part, kernel_part, gain_part), 'tm')]
    while x63 -> x35, local copies, waits for them, and re-layouts: 53.4 us -> 24.4 us
    slice x2, local copies, waits for them, and re-layouts: 1.47 us -> 27.1 us  [depthwise(): kernel_f[:, tap]]
    ppermute x44, starting transfers between devices: 20.5 us -> 44.6 us  [from_behind(): return lax.ppermute(block, axis, route)]
    concatenate x3, other arithmetic: 49.8 us -> 33 us  [per_device(): jnp.concatenate([first_half, second_half], axis=-1).astype(jnp.bfloat16)]
  transfers between devices with their start and end apart: 51 -> 51, of which waited for: 27 -> 30; matrix products, arithmetic and copies ran while one was open for 30% -> 31% of each run, Pallas kernels for 0% -> 0%
where the time goes in v1:
time: 667 us; the launch traced here: 655 us
  waiting for transfers between devices  248 us (37%)
  other arithmetic  145 us (22%)
  local copies, waits for them, and re-layouts  116 us (17%)
  matrix products  76.7 us (11%)
  starting transfers between devices  54 us (8%)
  between operations  15.7 us (2%)
    ppermute x44, waiting for transfers between devices, from_behind(): return lax.ppermute(block, axis, route)  179 us
    psum x1, waiting for transfers between devices, reduce_grads(): total = lax.psum(part, 'tm')  68 us
    ppermute x44, starting transfers between devices, from_behind(): return lax.ppermute(block, axis, route)  44.6 us
    reduce_sum x1, other arithmetic, norm_backward(): centre = mixed - jnp.mean(mixed, axis=-1, keepdims=True)  44.2 us
    reduce_sum x4, other arithmetic, tap_products(): jnp.sum(grad_f * padded[tap:tap + frame_rows].astype(jnp.float32), axis=0)  38 us
    concatenate x3, other arithmetic, per_device(): jnp.concatenate([first_half, second_half], axis=-1).astype(jnp.bfloat16)  33 us
    slice x2, local copies, waits for them, and re-layouts, depthwise(): kernel_f[:, tap]  27.1 us
    while x35, local copies, waits for them, and re-layouts  24.4 us
  transfers between devices with their start and end apart: 51, of which 30 were waited for; matrix products, arithmetic and copies ran while one was open for 31% of the time, Pallas kernels for 0%

profile of v1, /device:TPU:4, one launch (start us, length us, event | category | flops | bytes accessed | tf_op | source)
XLA Modules:
  0.0 654.7 jit_solution(10411791047309551320)
XLA Ops:
  17.3 5.2 collective-permute-start.8
  30.0 91.0 %while.48 = (s32[]{:T(128)}, bf16[384,2,128]{2,0,1:T(8,128)(2,1)}, bf16[384,2,128]{2,0,1:T(8,128)(2,1)}, f32[2,384]{1,0:T(2,128)S(1)}, f32[2,384]{1,0:T(2,128)S(...) while((s32[]{:T(128)}, bf16[384,2,128]{2,0,1:T(8,128)(2,1)}, ...), condition=%wide.region_3.4_spmd.clone, body=%wide.region_0.3_spmd.clone.sunk | while | flops 530552064 | bytes 7324782 | solution.py:188
  40.3 3.1 collective-permute-done.1
  63.4 3.6 collective-permute-done
  66.9 6.8 %collective-permute-done.1 = bf16[384,2,128]{2,0,1:T(8,128)(2,1)} collective-permute-done((bf16[384,2,128]{2,0,1:T(8,128)(2,1)}, bf16[384,2,128]{2,0,1:T(8,128)(2,1)}, u32[]{:S(2)}, u32[]{:S(2)}) %collective-permute-start.1) | collective-permute-done | bytes 196640 | tf_op jit(solution)/shard_map/while/body/eval_jaxpr/ppermute | solution.py:19
  88.5 3.0 fusion.256
  93.5 3.3 collective-permute-done.1
  100.6 3.0 fusion.256
  105.9 4.2 collective-permute-done.1
  126.1 3.1 slice.542
  130.9 3.2 reshape.233
  134.1 20.0 %slice_reduce_fusion.30 = (f32[2048]{0:T(1024)S(1)}, f32[2048]{0:T(1024)}, f32[2048]{0:T(1024)}, f32[2048]{0:T(1024)}, f32[2048]{0:T(1024)}, /*index=5*/f32[2048...) fusion(f32[2048,31]{1,0:T(8,128)} %reshape.233), kind=kLoop, calls=%fused_computation.384 | loop fusion | bytes 311296 | tf_op jit(solution)/shard_map/slice | solution.py:42
  154.1 7.2 %slice_reduce_fusion.29 = (f32[2048]{0:T(1024)}, f32[2048]{0:T(1024)}, f32[2048]{0:T(1024)}, f32[2048]{0:T(1024)}, f32[2048]{0:T(1024)}, /*index=5*/f32[2048]{0:...) fusion(f32[2048,31]{1,0:T(8,128)S(1)} %copy-done.2), kind=kLoop, calls=%fused_computation.383 | loop fusion | bytes 196608 | tf_op jit(solution)/shard_map/slice | solution.py:42
  166.4 44.2 %fusion.194 = (f32[384]{0:T(512)S(1)}, f32[384,2048]{1,0:T(8,128)S(1)}) fusion(f32[2048]{0:T(1024)} %get-tuple-element.684, bf16[15,2048]{1,0:T(8,128)(2,1)} %collective-permute-done.9, bf16[384,2048]{1,0:T(8,128)(2,1)} %copy-done.3, f32[2048]{0:T(1024)} %get-tuple-element.685, f32[2048]{0:T(1024)} %get-tuple-element.686, f32[2048]{0:T(1024)} %get-tuple-element.687, ...), kind=kLoop, calls=%fused_computation.412 | loop fusion | flops 143916672 | bytes 5096960 | tf_op jit(solution)/shard_map/reduce_sum | solution.py:69
  211.2 4.5 multiply_reduce_fusion.1
  217.8 20.1 %fusion.82 = (f32[2048]{0:T(1024)}, f32[2048]{0:T(1024)}, f32[2048]{0:T(1024)}, f32[2048]{0:T(1024)}, f32[2048]{0:T(1024)}, /*index=5*/f32[2048]{0:T(1024)}, f32...) fusion(bf16[15,2048]{1,0:T(8,128)(2,1)} %collective-permute-done.9, ...), kind=kLoop, calls=%fused_computation.218 | loop fusion | flops 49526784 | bytes 9586688 | tf_op jit(solution)/shard_map/reduce_sum | solution.py:61
  237.9 4.9 fusion.65
  242.8 7.3 %fusion.66 = (f32[2048]{0:T(1024)}, f32[2048]{0:T(1024)}, f32[2048]{0:T(1024)}, f32[2048]{0:T(1024)}, f32[2048]{0:T(1024)}, /*index=5*/f32[2048]{0:T(1024)}, f32[2048]{0:T(1024)}, f32[2048]{0:T(1024)}, f32[2048]{0:T(1024)}) fusion(bf16[384,2048]{1,0:T(8,128)(2,1)S(1)} %get-tuple-element.760, bf16[384,2048]{1,0:T(8,128)(2,1)S(1)} %copy-done.4, ...), kind=kLoop, calls=%fused_computation.202 | loop fusion | flops 43235328 | bytes 3280896 | tf_op jit(solution)/shard_map/reduce_sum | solution.py:61
  250.1 5.6 fusion.81
  255.7 6.1 stack.127
  268.3 5.4 copy.69
  279.5 4.2 pad_maximum_fusion
  283.7 8.8 %copy.70 = f32[32,136,256]{2,1,0:T(8,128)} copy(f32[32,136,256]{1,0,2:T(8,128)} %pad_maximum_fusion) | data formatting | bytes 8912896 | tf_op jit(solution)/shard_map/concatenate | solution.py:117
  293.4 228.3 %while.49 = (s32[]{:T(128)}, bf16[384,2,128]{2,0,1:T(8,128)(2,1)S(1)}, bf16[384,2,128]{2,0,1:T(8,128)(2,1)}, f32[384,2,128]{2,0,1:T(8,128)S(1)}, f32[384,2,128]{...) while((s32[]{:T(128)}, ...), condition=%wide.region_7.8_spmd.clone, body=%wide.region_6.7_spmd.clone.sunk | while | flops 380240640 | bytes 14556372 | solution.py:237
  300.5 3.2 collective-permute-start.3
  304.8 11.6 %collective-permute-done.2 = bf16[384,2,128]{2,0,1:T(8,128)(2,1)S(1)} collective-permute-done((bf16[384,2,128]{2,0,1:T(8,128)(2,1)S(1)}, bf16[384,2,128]{2,0,1:T(8,128)(2,1)S(1)}, u32[]{:S(2)}, u32[]{:S(2)}) %collective-permute-start.2) | collective-permute-done | bytes 196640 | tf_op jit(solution)/shard_map/while/body/eval_jaxpr/ppermute | solution.py:19
  316.4 3.2 collective-permute-done.3
  326.8 3.2 collective-permute-start.3
  332.1 9.6 %collective-permute-done.2 = bf16[384,2,128]{2,0,1:T(8,128)(2,1)S(1)} collective-permute-done((bf16[384,2,128]{2,0,1:T(8,128)(2,1)S(1)}, bf16[384,2,128]{2,0,1:T(8,128)(2,1)S(1)}, u32[]{:S(2)}, u32[]{:S(2)}) %collective-permute-start.2) | collective-permute-done | bytes 196640 | tf_op jit(solution)/shard_map/while/body/eval_jaxpr/ppermute | solution.py:19
  341.7 4.2 collective-permute-done.3
  353.9 3.5 collective-permute-start.3
  359.4 26.4 %collective-permute-done.2 = bf16[384,2,128]{2,0,1:T(8,128)(2,1)S(1)} collective-permute-done((bf16[384,2,128]{2,0,1:T(8,128)(2,1)S(1)}, bf16[384,2,128]{2,0,1:T(8,128)(2,1)S(1)}, u32[]{:S(2)}, u32[]{:S(2)}) %collective-permute-start.2) | collective-permute-done | bytes 196640 | tf_op jit(solution)/shard_map/while/body/eval_jaxpr/ppermute | solution.py:19
  385.8 4.3 collective-permute-done.3
  397.7 3.5 collective-permute-start.3
  403.3 17.0 %collective-permute-done.2 = bf16[384,2,128]{2,0,1:T(8,128)(2,1)S(1)} collective-permute-done((bf16[384,2,128]{2,0,1:T(8,128)(2,1)S(1)}, bf16[384,2,128]{2,0,1:T(8,128)(2,1)S(1)}, u32[]{:S(2)}, u32[]{:S(2)}) %collective-permute-start.2) | collective-permute-done | bytes 196640 | tf_op jit(solution)/shard_map/while/body/eval_jaxpr/ppermute | solution.py:19
  420.3 4.3 collective-permute-done.3
  432.3 3.5 collective-permute-start.3
  437.9 16.5 %collective-permute-done.2 = bf16[384,2,128]{2,0,1:T(8,128)(2,1)S(1)} collective-permute-done((bf16[384,2,128]{2,0,1:T(8,128)(2,1)S(1)}, bf16[384,2,128]{2,0,1:T(8,128)(2,1)S(1)}, u32[]{:S(2)}, u32[]{:S(2)}) %collective-permute-start.2) | collective-permute-done | bytes 196640 | tf_op jit(solution)/shard_map/while/body/eval_jaxpr/ppermute | solution.py:19
  454.4 4.3 collective-permute-done.3
  466.5 3.5 collective-permute-start.3
  472.0 17.6 %collective-permute-done.2 = bf16[384,2,128]{2,0,1:T(8,128)(2,1)S(1)} collective-permute-done((bf16[384,2,128]{2,0,1:T(8,128)(2,1)S(1)}, bf16[384,2,128]{2,0,1:T(8,128)(2,1)S(1)}, u32[]{:S(2)}, u32[]{:S(2)}) %collective-permute-start.2) | collective-permute-done | bytes 196640 | tf_op jit(solution)/shard_map/while/body/eval_jaxpr/ppermute | solution.py:19
  489.6 4.3 collective-permute-done.3
  499.8 3.5 collective-permute-start.3
  505.4 13.1 %collective-permute-done.2 = bf16[384,2,128]{2,0,1:T(8,128)(2,1)S(1)} collective-permute-done((bf16[384,2,128]{2,0,1:T(8,128)(2,1)S(1)}, bf16[384,2,128]{2,0,1:T(8,128)(2,1)S(1)}, u32[]{:S(2)}, u32[]{:S(2)}) %collective-permute-start.2) | collective-permute-done | bytes 196640 | tf_op jit(solution)/shard_map/while/body/eval_jaxpr/ppermute | solution.py:19
  518.5 3.2 collective-permute-done.3
  539.4 26.6 %fusion.108 = (bf16[1,384,2048]{2,1,0:T(8,128)(2,1)}, f32[384,2048]{1,0:T(8,128)S(1)}) fusion(bf16[384,4096]{1,0:T(8,128)(2,1)} %bitcast.195, f32[384]{0:T(512)S(1)} %fusion.187, f32[2048]{0:T(1024)S(1)} %copy-done.19, bf16[384,2048]{1,0:T(8,128)(2,1)S(1)} %copy-done.7, bf16[15,2048]{1,0:T(8,128)(2,1)S(1)} %collective-permute-done.11, ...), kind=kLoop, calls=%fused_computation.252 | loop fusion | flops 148635648 | bytes 8242688 | tf_op jit(solution)/shard_map/concatenate | solution.py:267
  568.3 4.1 pad_maximum_fusion.1
  576.0 68.0 %all-reduce.2.cloned.1.call-done = f32[136,256]{1,0:T(8,128)} async-done(((f32[136,256]{1,0:T(8,128)}), f32[136,256]{1,0:T(8,128)}) %all-reduce.2.cloned.1.call-update) | async-done | bytes 139280 | tf_op jit(solution)/shard_map/psum | solution.py:119
  (371 shorter events, 199.8 us)
Async XLA Ops:
  7.2 118.9 %all-gather.3.cloned.1.call-start = ((), (), s32[]{:S(2)}) async-start(), calls=%async_computation.3 | async-start | bytes 2297856 | tf_op jit(solution)/shard_map/all_gather | solution.py:93
  10.6 557.7 %reduce-scatter.2.cloned.1.call-start = ((), (), s32[]{:S(2)}) async-start(), calls=%async_computation.1 | async-start | bytes 4595712 | tf_op jit(solution)/shard_map/reduce_scatter | solution.py:118
  16.0 150.4 %collective-permute-start.9 = (bf16[15,2048]{1,0:T(8,128)(2,1)}, bf16[15,2048]{1,0:T(8,128)(2,1)}, u32[]{:S(2)}, u32[]{:S(2)}) collective-permute-start(bf16[15,2048]{1,0:T(8,128)(2,1)} %get-tuple-element.771), channel_id=1, source_target_pairs={{1,0},{2,1},{3,2},{4,3},{5,4},{6,5},{7,6},{9,8},{10,9},{11,10},{12... | collective-permute-start | bytes 184328 | tf_op jit(solution)/shard_map/ppermute | solution.py:32
  17.3 149.1 %collective-permute-start.8 = (bf16[15,2048]{1,0:T(8,128)(2,1)}, bf16[15,2048]{1,0:T(8,128)(2,1)}, u32[]{:S(2)}, u32[]{:S(2)}) collective-permute-start(bf16[15,2048]{1,0:T(8,128)(2,1)} %get-tuple-element.770), channel_id=1, source_target_pairs={{0,1},{1,2},{2,3},{3,4},{4,5},{5,6},{6,7},{8,9},{9,10},{10,11},{11... | collective-permute-start | bytes 184328 | tf_op jit(solution)/shard_map/ppermute | solution.py:30
  30.9 9.4 %collective-permute-start = (bf16[384,2,128]{2,0,1:T(8,128)(2,1)S(1)}, bf16[384,2,128]{2,0,1:T(8,128)(2,1)}, u32[]{:S(2)}, u32[]{:S(2)}) collective-permute-start(bf16[384,2,128]{2,0,1:T(8,128)(2,1)S(1)} %copy.107), channel_id=1, source_target_pairs={{7,0},{0,1},{1,2},{2,3},{3,4},{4,5},{5,6},{6,7},{15,8},{8,9},{9,10... | collective-permute-start | bytes 589832 | tf_op jit(solution)/shard_map/while/body/eval_jaxpr/ppermute | solution.py:19
  34.1 9.3 %collective-permute-start.1 = (bf16[384,2,128]{2,0,1:T(8,128)(2,1)}, bf16[384,2,128]{2,0,1:T(8,128)(2,1)}, u32[]{:S(2)}, u32[]{:S(2)}) collective-permute-start(bf16[384,2,128]{2,0,1:T(8,128)(2,1)} %copy.108), channel_id=1, source_target_pairs={{7,0},{0,1},{1,2},{2,3},{3,4},{4,5},{5,6},{6,7},{15,8},{8,9},{9,10... | collective-permute-start | bytes 589832 | tf_op jit(solution)/shard_map/while/body/eval_jaxpr/ppermute | solution.py:19
  44.4 10.0 %collective-permute-start = (bf16[384,2,128]{2,0,1:T(8,128)(2,1)S(1)}, bf16[384,2,128]{2,0,1:T(8,128)(2,1)}, u32[]{:S(2)}, u32[]{:S(2)}) collective-permute-start(bf16[384,2,128]{2,0,1:T(8,128)(2,1)S(1)} %copy.107), channel_id=1, source_target_pairs={{7,0},{0,1},{1,2},{2,3},{3,4},{4,5},{5,6},{6,7},{15,8},{8,9},{9,10... | collective-permute-start | bytes 589832 | tf_op jit(solution)/shard_map/while/body/eval_jaxpr/ppermute | solution.py:19
  46.0 10.6 %collective-permute-start.1 = (bf16[384,2,128]{2,0,1:T(8,128)(2,1)}, bf16[384,2,128]{2,0,1:T(8,128)(2,1)}, u32[]{:S(2)}, u32[]{:S(2)}) collective-permute-start(bf16[384,2,128]{2,0,1:T(8,128)(2,1)} %copy.108), channel_id=1, source_target_pairs={{7,0},{0,1},{1,2},{2,3},{3,4},{4,5},{5,6},{6,7},{15,8},{8,9},{9,10... | collective-permute-start | bytes 589832 | tf_op jit(solution)/shard_map/while/body/eval_jaxpr/ppermute | solution.py:19
  57.5 9.4 %collective-permute-start = (bf16[384,2,128]{2,0,1:T(8,128)(2,1)S(1)}, bf16[384,2,128]{2,0,1:T(8,128)(2,1)}, u32[]{:S(2)}, u32[]{:S(2)}) collective-permute-start(bf16[384,2,128]{2,0,1:T(8,128)(2,1)S(1)} %copy.107), channel_id=1, source_target_pairs={{7,0},{0,1},{1,2},{2,3},{3,4},{4,5},{5,6},{6,7},{15,8},{8,9},{9,10... | collective-permute-start | bytes 589832 | tf_op jit(solution)/shard_map/while/body/eval_jaxpr/ppermute | solution.py:19
  59.1 14.6 %collective-permute-start.1 = (bf16[384,2,128]{2,0,1:T(8,128)(2,1)}, bf16[384,2,128]{2,0,1:T(8,128)(2,1)}, u32[]{:S(2)}, u32[]{:S(2)}) collective-permute-start(bf16[384,2,128]{2,0,1:T(8,128)(2,1)} %copy.108), channel_id=1, source_target_pairs={{7,0},{0,1},{1,2},{2,3},{3,4},{4,5},{5,6},{6,7},{15,8},{8,9},{9,10... | collective-permute-start | bytes 589832 | tf_op jit(solution)/shard_map/while/body/eval_jaxpr/ppermute | solution.py:19
  74.7 7.9 %collective-permute-start = (bf16[384,2,128]{2,0,1:T(8,128)(2,1)S(1)}, bf16[384,2,128]{2,0,1:T(8,128)(2,1)}, u32[]{:S(2)}, u32[]{:S(2)}) collective-permute-start(bf16[384,2,128]{2,0,1:T(8,128)(2,1)S(1)} %copy.107), channel_id=1, source_target_pairs={{7,0},{0,1},{1,2},{2,3},{3,4},{4,5},{5,6},{6,7},{15,8},{8,9},{9,10... | collective-permute-start | bytes 589832 | tf_op jit(solution)/shard_map/while/body/eval_jaxpr/ppermute | solution.py:19
  76.3 8.4 %collective-permute-start.1 = (bf16[384,2,128]{2,0,1:T(8,128)(2,1)}, bf16[384,2,128]{2,0,1:T(8,128)(2,1)}, u32[]{:S(2)}, u32[]{:S(2)}) collective-permute-start(bf16[384,2,128]{2,0,1:T(8,128)(2,1)} %copy.108), channel_id=1, source_target_pairs={{7,0},{0,1},{1,2},{2,3},{3,4},{4,5},{5,6},{6,7},{15,8},{8,9},{9,10... | collective-permute-start | bytes 589832 | tf_op jit(solution)/shard_map/while/body/eval_jaxpr/ppermute | solution.py:19
  85.6 7.9 %collective-permute-start = (bf16[384,2,128]{2,0,1:T(8,128)(2,1)S(1)}, bf16[384,2,128]{2,0,1:T(8,128)(2,1)}, u32[]{:S(2)}, u32[]{:S(2)}) collective-permute-start(bf16[384,2,128]{2,0,1:T(8,128)(2,1)S(1)} %copy.107), channel_id=1, source_target_pairs={{7,0},{0,1},{1,2},{2,3},{3,4},{4,5},{5,6},{6,7},{15,8},{8,9},{9,10... | collective-permute-start | bytes 589832 | tf_op jit(solution)/shard_map/while/body/eval_jaxpr/ppermute | solution.py:19
  87.3 9.6 %collective-permute-start.1 = (bf16[384,2,128]{2,0,1:T(8,128)(2,1)}, bf16[384,2,128]{2,0,1:T(8,128)(2,1)}, u32[]{:S(2)}, u32[]{:S(2)}) collective-permute-start(bf16[384,2,128]{2,0,1:T(8,128)(2,1)} %copy.108), channel_id=1, source_target_pairs={{7,0},{0,1},{1,2},{2,3},{3,4},{4,5},{5,6},{6,7},{15,8},{8,9},{9,10... | collective-permute-start | bytes 589832 | tf_op jit(solution)/shard_map/while/body/eval_jaxpr/ppermute | solution.py:19
  97.7 8.1 %collective-permute-start = (bf16[384,2,128]{2,0,1:T(8,128)(2,1)S(1)}, bf16[384,2,128]{2,0,1:T(8,128)(2,1)}, u32[]{:S(2)}, u32[]{:S(2)}) collective-permute-start(bf16[384,2,128]{2,0,1:T(8,128)(2,1)S(1)} %copy.107), channel_id=1, source_target_pairs={{7,0},{0,1},{1,2},{2,3},{3,4},{4,5},{5,6},{6,7},{15,8},{8,9},{9,10... | collective-permute-start | bytes 589832 | tf_op jit(solution)/shard_map/while/body/eval_jaxpr/ppermute | solution.py:19
  99.4 10.7 %collective-permute-start.1 = (bf16[384,2,128]{2,0,1:T(8,128)(2,1)}, bf16[384,2,128]{2,0,1:T(8,128)(2,1)}, u32[]{:S(2)}, u32[]{:S(2)}) collective-permute-start(bf16[384,2,128]{2,0,1:T(8,128)(2,1)} %copy.108), channel_id=1, source_target_pairs={{7,0},{0,1},{1,2},{2,3},{3,4},{4,5},{5,6},{6,7},{15,8},{8,9},{9,10... | collective-permute-start | bytes 589832 | tf_op jit(solution)/shard_map/while/body/eval_jaxpr/ppermute | solution.py:19
  112.6 8.4 %collective-permute-start.1 = (bf16[384,2,128]{2,0,1:T(8,128)(2,1)}, bf16[384,2,128]{2,0,1:T(8,128)(2,1)}, u32[]{:S(2)}, u32[]{:S(2)}) collective-permute-start(bf16[384,2,128]{2,0,1:T(8,128)(2,1)} %copy.108), channel_id=1, source_target_pairs={{7,0},{0,1},{1,2},{2,3},{3,4},{4,5},{5,6},{6,7},{15,8},{8,9},{9,10... | collective-permute-start | bytes 589832 | tf_op jit(solution)/shard_map/while/body/eval_jaxpr/ppermute | solution.py:19
  292.5 351.6 %all-reduce.2.cloned.1.call-start = ((), (), s32[]{:S(2)}) async-start(), calls=%async_computation.2 | async-start | bytes 278528 | tf_op jit(solution)/shard_map/psum | solution.py:119
  297.5 22.1 %collective-permute-start.4 = (f32[384,2,128]{2,0,1:T(8,128)}, f32[384,2,128]{2,0,1:T(8,128)S(1)}, u32[]{:S(2)}, u32[]{:S(2)}) collective-permute-start(f32[384,2,128]{2,0,1:T(8,128)} %fusion.269), channel_id=1, source_target_pairs={{7,0},{0,1},{1,2},{2,3},{3,4},{4,5},{5,6},{6,7},{15,8},{8,9},{9,10... | collective-permute-start | bytes 1179656 | tf_op jit(solution)/shard_map/while/body/eval_jaxpr/ppermute | solution.py:19
  298.7 21.0 %collective-permute-start.5 = (f32[384,2,128]{2,0,1:T(8,128)}, f32[384,2,128]{2,0,1:T(8,128)S(1)}, u32[]{:S(2)}, u32[]{:S(2)}) collective-permute-start(f32[384,2,128]{2,0,1:T(8,128)} %fusion.270), channel_id=1, source_target_pairs={{7,0},{0,1},{1,2},{2,3},{3,4},{4,5},{5,6},{6,7},{15,8},{8,9},{9,10... | collective-permute-start | bytes 1179656 | tf_op jit(solution)/shard_map/while/body/eval_jaxpr/ppermute | solution.py:19
  298.7 17.7 %collective-permute-start.2 = (bf16[384,2,128]{2,0,1:T(8,128)(2,1)S(1)}, bf16[384,2,128]{2,0,1:T(8,128)(2,1)S(1)}, u32[]{:S(2)}, u32[]{:S(2)}) collective-permute-start(bf16[384,2,128]{2,0,1:T(8,128)(2,1)S(1)} %copy.125), channel_id=1, source_target_pairs={{7,0},{0,1},{1,2},{2,3},{3,4},{4,5},{5,6},{6,7},{15,8},{8,9},{9,10... | collective-permute-start | bytes 589832 | tf_op jit(solution)/shard_map/while/body/eval_jaxpr/ppermute | solution.py:19
  300.5 19.1 %collective-permute-start.3 = (bf16[384,2,128]{2,0,1:T(8,128)(2,1)S(1)}, bf16[384,2,128]{2,0,1:T(8,128)(2,1)}, u32[]{:S(2)}, u32[]{:S(2)}) collective-permute-start(bf16[384,2,128]{2,0,1:T(8,128)(2,1)S(1)} %copy.126), channel_id=1, source_target_pairs={{7,0},{0,1},{1,2},{2,3},{3,4},{4,5},{5,6},{6,7},{15,8},{8,9},{9,10... | collective-permute-start | bytes 589832 | tf_op jit(solution)/shard_map/while/body/eval_jaxpr/ppermute | solution.py:19
  323.8 22.1 %collective-permute-start.4 = (f32[384,2,128]{2,0,1:T(8,128)}, f32[384,2,128]{2,0,1:T(8,128)S(1)}, u32[]{:S(2)}, u32[]{:S(2)}) collective-permute-start(f32[384,2,128]{2,0,1:T(8,128)} %fusion.269), channel_id=1, source_target_pairs={{7,0},{0,1},{1,2},{2,3},{3,4},{4,5},{5,6},{6,7},{15,8},{8,9},{9,10... | collective-permute-start | bytes 1179656 | tf_op jit(solution)/shard_map/while/body/eval_jaxpr/ppermute | solution.py:19
  324.9 21.0 %collective-permute-start.5 = (f32[384,2,128]{2,0,1:T(8,128)}, f32[384,2,128]{2,0,1:T(8,128)S(1)}, u32[]{:S(2)}, u32[]{:S(2)}) collective-permute-start(f32[384,2,128]{2,0,1:T(8,128)} %fusion.270), channel_id=1, source_target_pairs={{7,0},{0,1},{1,2},{2,3},{3,4},{4,5},{5,6},{6,7},{15,8},{8,9},{9,10... | collective-permute-start | bytes 1179656 | tf_op jit(solution)/shard_map/while/body/eval_jaxpr/ppermute | solution.py:19
  324.9 16.8 %collective-permute-start.2 = (bf16[384,2,128]{2,0,1:T(8,128)(2,1)S(1)}, bf16[384,2,128]{2,0,1:T(8,128)(2,1)S(1)}, u32[]{:S(2)}, u32[]{:S(2)}) collective-permute-start(bf16[384,2,128]{2,0,1:T(8,128)(2,1)S(1)} %copy.125), channel_id=1, source_target_pairs={{7,0},{0,1},{1,2},{2,3},{3,4},{4,5},{5,6},{6,7},{15,8},{8,9},{9,10... | collective-permute-start | bytes 589832 | tf_op jit(solution)/shard_map/while/body/eval_jaxpr/ppermute | solution.py:19
  326.8 19.1 %collective-permute-start.3 = (bf16[384,2,128]{2,0,1:T(8,128)(2,1)S(1)}, bf16[384,2,128]{2,0,1:T(8,128)(2,1)}, u32[]{:S(2)}, u32[]{:S(2)}) collective-permute-start(bf16[384,2,128]{2,0,1:T(8,128)(2,1)S(1)} %copy.126), channel_id=1, source_target_pairs={{7,0},{0,1},{1,2},{2,3},{3,4},{4,5},{5,6},{6,7},{15,8},{8,9},{9,10... | collective-permute-start | bytes 589832 | tf_op jit(solution)/shard_map/while/body/eval_jaxpr/ppermute | solution.py:19
  350.0 40.1 %collective-permute-start.4 = (f32[384,2,128]{2,0,1:T(8,128)}, f32[384,2,128]{2,0,1:T(8,128)S(1)}, u32[]{:S(2)}, u32[]{:S(2)}) collective-permute-start(f32[384,2,128]{2,0,1:T(8,128)} %fusion.269), channel_id=1, source_target_pairs={{7,0},{0,1},{1,2},{2,3},{3,4},{4,5},{5,6},{6,7},{15,8},{8,9},{9,10... | collective-permute-start | bytes 1179656 | tf_op jit(solution)/shard_map/while/body/eval_jaxpr/ppermute | solution.py:19
  351.1 39.0 %collective-permute-start.5 = (f32[384,2,128]{2,0,1:T(8,128)}, f32[384,2,128]{2,0,1:T(8,128)S(1)}, u32[]{:S(2)}, u32[]{:S(2)}) collective-permute-start(f32[384,2,128]{2,0,1:T(8,128)} %fusion.270), channel_id=1, source_target_pairs={{7,0},{0,1},{1,2},{2,3},{3,4},{4,5},{5,6},{6,7},{15,8},{8,9},{9,10... | collective-permute-start | bytes 1179656 | tf_op jit(solution)/shard_map/while/body/eval_jaxpr/ppermute | solution.py:19
  351.1 34.7 %collective-permute-start.2 = (bf16[384,2,128]{2,0,1:T(8,128)(2,1)S(1)}, bf16[384,2,128]{2,0,1:T(8,128)(2,1)S(1)}, u32[]{:S(2)}, u32[]{:S(2)}) collective-permute-start(bf16[384,2,128]{2,0,1:T(8,128)(2,1)S(1)} %copy.125), channel_id=1, source_target_pairs={{7,0},{0,1},{1,2},{2,3},{3,4},{4,5},{5,6},{6,7},{15,8},{8,9},{9,10... | collective-permute-start | bytes 589832 | tf_op jit(solution)/shard_map/while/body/eval_jaxpr/ppermute | solution.py:19
  353.9 36.3 %collective-permute-start.3 = (bf16[384,2,128]{2,0,1:T(8,128)(2,1)S(1)}, bf16[384,2,128]{2,0,1:T(8,128)(2,1)}, u32[]{:S(2)}, u32[]{:S(2)}) collective-permute-start(bf16[384,2,128]{2,0,1:T(8,128)(2,1)S(1)} %copy.126), channel_id=1, source_target_pairs={{7,0},{0,1},{1,2},{2,3},{3,4},{4,5},{5,6},{6,7},{15,8},{8,9},{9,10... | collective-permute-start | bytes 589832 | tf_op jit(solution)/shard_map/while/body/eval_jaxpr/ppermute | solution.py:19
  394.3 30.3 %collective-permute-start.4 = (f32[384,2,128]{2,0,1:T(8,128)}, f32[384,2,128]{2,0,1:T(8,128)S(1)}, u32[]{:S(2)}, u32[]{:S(2)}) collective-permute-start(f32[384,2,128]{2,0,1:T(8,128)} %fusion.269), channel_id=1, source_target_pairs={{7,0},{0,1},{1,2},{2,3},{3,4},{4,5},{5,6},{6,7},{15,8},{8,9},{9,10... | collective-permute-start | bytes 1179656 | tf_op jit(solution)/shard_map/while/body/eval_jaxpr/ppermute | solution.py:19
  395.4 29.2 %collective-permute-start.5 = (f32[384,2,128]{2,0,1:T(8,128)}, f32[384,2,128]{2,0,1:T(8,128)S(1)}, u32[]{:S(2)}, u32[]{:S(2)}) collective-permute-start(f32[384,2,128]{2,0,1:T(8,128)} %fusion.270), channel_id=1, source_target_pairs={{7,0},{0,1},{1,2},{2,3},{3,4},{4,5},{5,6},{6,7},{15,8},{8,9},{9,10... | collective-permute-start | bytes 1179656 | tf_op jit(solution)/shard_map/while/body/eval_jaxpr/ppermute | solution.py:19
  395.4 24.9 %collective-permute-start.2 = (bf16[384,2,128]{2,0,1:T(8,128)(2,1)S(1)}, bf16[384,2,128]{2,0,1:T(8,128)(2,1)S(1)}, u32[]{:S(2)}, u32[]{:S(2)}) collective-permute-start(bf16[384,2,128]{2,0,1:T(8,128)(2,1)S(1)} %copy.125), channel_id=1, source_target_pairs={{7,0},{0,1},{1,2},{2,3},{3,4},{4,5},{5,6},{6,7},{15,8},{8,9},{9,10... | collective-permute-start | bytes 589832 | tf_op jit(solution)/shard_map/while/body/eval_jaxpr/ppermute | solution.py:19
  397.7 26.9 %collective-permute-start.3 = (bf16[384,2,128]{2,0,1:T(8,128)(2,1)S(1)}, bf16[384,2,128]{2,0,1:T(8,128)(2,1)}, u32[]{:S(2)}, u32[]{:S(2)}) collective-permute-start(bf16[384,2,128]{2,0,1:T(8,128)(2,1)S(1)} %copy.126), channel_id=1, source_target_pairs={{7,0},{0,1},{1,2},{2,3},{3,4},{4,5},{5,6},{6,7},{15,8},{8,9},{9,10... | collective-permute-start | bytes 589832 | tf_op jit(solution)/shard_map/while/body/eval_jaxpr/ppermute | solution.py:19
  428.7 30.0 %collective-permute-start.4 = (f32[384,2,128]{2,0,1:T(8,128)}, f32[384,2,128]{2,0,1:T(8,128)S(1)}, u32[]{:S(2)}, u32[]{:S(2)}) collective-permute-start(f32[384,2,128]{2,0,1:T(8,128)} %fusion.269), channel_id=1, source_target_pairs={{7,0},{0,1},{1,2},{2,3},{3,4},{4,5},{5,6},{6,7},{15,8},{8,9},{9,10... | collective-permute-start | bytes 1179656 | tf_op jit(solution)/shard_map/while/body/eval_jaxpr/ppermute | solution.py:19
  429.9 28.8 %collective-permute-start.5 = (f32[384,2,128]{2,0,1:T(8,128)}, f32[384,2,128]{2,0,1:T(8,128)S(1)}, u32[]{:S(2)}, u32[]{:S(2)}) collective-permute-start(f32[384,2,128]{2,0,1:T(8,128)} %fusion.270), channel_id=1, source_target_pairs={{7,0},{0,1},{1,2},{2,3},{3,4},{4,5},{5,6},{6,7},{15,8},{8,9},{9,10... | collective-permute-start | bytes 1179656 | tf_op jit(solution)/shard_map/while/body/eval_jaxpr/ppermute | solution.py:19
  429.9 24.5 %collective-permute-start.2 = (bf16[384,2,128]{2,0,1:T(8,128)(2,1)S(1)}, bf16[384,2,128]{2,0,1:T(8,128)(2,1)S(1)}, u32[]{:S(2)}, u32[]{:S(2)}) collective-permute-start(bf16[384,2,128]{2,0,1:T(8,128)(2,1)S(1)} %copy.125), channel_id=1, source_target_pairs={{7,0},{0,1},{1,2},{2,3},{3,4},{4,5},{5,6},{6,7},{15,8},{8,9},{9,10... | collective-permute-start | bytes 589832 | tf_op jit(solution)/shard_map/while/body/eval_jaxpr/ppermute | solution.py:19
  432.3 26.4 %collective-permute-start.3 = (bf16[384,2,128]{2,0,1:T(8,128)(2,1)S(1)}, bf16[384,2,128]{2,0,1:T(8,128)(2,1)}, u32[]{:S(2)}, u32[]{:S(2)}) collective-permute-start(bf16[384,2,128]{2,0,1:T(8,128)(2,1)S(1)} %copy.126), channel_id=1, source_target_pairs={{7,0},{0,1},{1,2},{2,3},{3,4},{4,5},{5,6},{6,7},{15,8},{8,9},{9,10... | collective-permute-start | bytes 589832 | tf_op jit(solution)/shard_map/while/body/eval_jaxpr/ppermute | solution.py:19
  462.8 31.1 %collective-permute-start.4 = (f32[384,2,128]{2,0,1:T(8,128)}, f32[384,2,128]{2,0,1:T(8,128)S(1)}, u32[]{:S(2)}, u32[]{:S(2)}) collective-permute-start(f32[384,2,128]{2,0,1:T(8,128)} %fusion.269), channel_id=1, source_target_pairs={{7,0},{0,1},{1,2},{2,3},{3,4},{4,5},{5,6},{6,7},{15,8},{8,9},{9,10... | collective-permute-start | bytes 1179656 | tf_op jit(solution)/shard_map/while/body/eval_jaxpr/ppermute | solution.py:19
  464.0 30.0 %collective-permute-start.5 = (f32[384,2,128]{2,0,1:T(8,128)}, f32[384,2,128]{2,0,1:T(8,128)S(1)}, u32[]{:S(2)}, u32[]{:S(2)}) collective-permute-start(f32[384,2,128]{2,0,1:T(8,128)} %fusion.270), channel_id=1, source_target_pairs={{7,0},{0,1},{1,2},{2,3},{3,4},{4,5},{5,6},{6,7},{15,8},{8,9},{9,10... | collective-permute-start | bytes 1179656 | tf_op jit(solution)/shard_map/while/body/eval_jaxpr/ppermute | solution.py:19
  464.0 25.7 %collective-permute-start.2 = (bf16[384,2,128]{2,0,1:T(8,128)(2,1)S(1)}, bf16[384,2,128]{2,0,1:T(8,128)(2,1)S(1)}, u32[]{:S(2)}, u32[]{:S(2)}) collective-permute-start(bf16[384,2,128]{2,0,1:T(8,128)(2,1)S(1)} %copy.125), channel_id=1, source_target_pairs={{7,0},{0,1},{1,2},{2,3},{3,4},{4,5},{5,6},{6,7},{15,8},{8,9},{9,10... | collective-permute-start | bytes 589832 | tf_op jit(solution)/shard_map/while/body/eval_jaxpr/ppermute | solution.py:19
  466.5 27.5 %collective-permute-start.3 = (bf16[384,2,128]{2,0,1:T(8,128)(2,1)S(1)}, bf16[384,2,128]{2,0,1:T(8,128)(2,1)}, u32[]{:S(2)}, u32[]{:S(2)}) collective-permute-start(bf16[384,2,128]{2,0,1:T(8,128)(2,1)S(1)} %copy.126), channel_id=1, source_target_pairs={{7,0},{0,1},{1,2},{2,3},{3,4},{4,5},{5,6},{6,7},{15,8},{8,9},{9,10... | collective-permute-start | bytes 589832 | tf_op jit(solution)/shard_map/while/body/eval_jaxpr/ppermute | solution.py:19
  498.1 23.5 %collective-permute-start.4 = (f32[384,2,128]{2,0,1:T(8,128)}, f32[384,2,128]{2,0,1:T(8,128)S(1)}, u32[]{:S(2)}, u32[]{:S(2)}) collective-permute-start(f32[384,2,128]{2,0,1:T(8,128)} %fusion.269), channel_id=1, source_target_pairs={{7,0},{0,1},{1,2},{2,3},{3,4},{4,5},{5,6},{6,7},{15,8},{8,9},{9,10... | collective-permute-start | bytes 1179656 | tf_op jit(solution)/shard_map/while/body/eval_jaxpr/ppermute | solution.py:19
  499.2 22.4 %collective-permute-start.5 = (f32[384,2,128]{2,0,1:T(8,128)}, f32[384,2,128]{2,0,1:T(8,128)S(1)}, u32[]{:S(2)}, u32[]{:S(2)}) collective-permute-start(f32[384,2,128]{2,0,1:T(8,128)} %fusion.270), channel_id=1, source_target_pairs={{7,0},{0,1},{1,2},{2,3},{3,4},{4,5},{5,6},{6,7},{15,8},{8,9},{9,10... | collective-permute-start | bytes 1179656 | tf_op jit(solution)/shard_map/while/body/eval_jaxpr/ppermute | solution.py:19
  499.2 19.2 %collective-permute-start.2 = (bf16[384,2,128]{2,0,1:T(8,128)(2,1)S(1)}, bf16[384,2,128]{2,0,1:T(8,128)(2,1)S(1)}, u32[]{:S(2)}, u32[]{:S(2)}) collective-permute-start(bf16[384,2,128]{2,0,1:T(8,128)(2,1)S(1)} %copy.125), channel_id=1, source_target_pairs={{7,0},{0,1},{1,2},{2,3},{3,4},{4,5},{5,6},{6,7},{15,8},{8,9},{9,10... | collective-permute-start | bytes 589832 | tf_op jit(solution)/shard_map/while/body/eval_jaxpr/ppermute | solution.py:19
  499.8 21.9 %collective-permute-start.3 = (bf16[384,2,128]{2,0,1:T(8,128)(2,1)S(1)}, bf16[384,2,128]{2,0,1:T(8,128)(2,1)}, u32[]{:S(2)}, u32[]{:S(2)}) collective-permute-start(bf16[384,2,128]{2,0,1:T(8,128)(2,1)S(1)} %copy.126), channel_id=1, source_target_pairs={{7,0},{0,1},{1,2},{2,3},{3,4},{4,5},{5,6},{6,7},{15,8},{8,9},{9,10... | collective-permute-start | bytes 589832 | tf_op jit(solution)/shard_map/while/body/eval_jaxpr/ppermute | solution.py:19
  531.4 40.9 %collective-permute-start.6 = (bf16[384,2,128]{2,0,1:T(8,128)(2,1)}, bf16[384,2,128]{2,0,1:T(8,128)(2,1)}, u32[]{:S(2)}, u32[]{:S(2)}) collective-permute-start(bf16[384,2,128]{2,0,1:T(8,128)(2,1)} %fusion.174), channel_id=1, source_target_pairs={{7,0},{0,1},{1,2},{2,3},{3,4},{4,5},{5,6},{6,7},{15,8},{8,9},{9,10... | collective-permute-start | bytes 589832 | tf_op jit(solution)/shard_map/ppermute | solution.py:19
  536.3 38.0 %collective-permute-start.7 = (bf16[384,2,128]{0,2,1:T(8,128)(2,1)S(1)}, bf16[384,2,128]{0,2,1:T(8,128)(2,1)}, u32[]{:S(2)}, u32[]{:S(2)}) collective-permute-start(bf16[384,2,128]{0,2,1:T(8,128)(2,1)S(1)} %fusion.175), channel_id=1, source_target_pairs={{7,0},{0,1},{1,2},{2,3},{3,4},{4,5},{5,6},{6,7},{15,8},{8,9},{9,10... | collective-permute-start | bytes 589832 | tf_op jit(solution)/shard_map/ppermute | solution.py:19
  (58 other events, 830.2 us)
Sparse Core Ops, SparseCore 0:
  10.7 84.6 all-gather.2
  292.6 146.4 reduce-scatter.1
  568.4 75.5 all-reduce.1

commit v2 on v1

--- a/solution.py
+++ b/solution.py
@@ -104,25 +104,36 @@
 def reduce_grads(proj_term, kernel_term, gain_term):
     count = lax.axis_size("dp")
     width = proj_term.shape[1]
-    proj_blocks = proj_term.reshape(count, -1, width)
-    proj_rows = proj_blocks.shape[1]
+    proj_part = lax.psum_scatter(proj_term, "dp", scatter_dimension=0, tiled=True)
     kernel_blocks = kernel_term.reshape(count, -1)
     gain_blocks = gain_term.reshape(count, -1)
     tail = jnp.concatenate([kernel_blocks, gain_blocks], axis=1)
     tail_cols = tail.shape[1]
     tail_rows = -(-tail_cols // width)
-    tail = jnp.pad(tail, ((0, 0), (0, tail_rows * width - tail_cols))).reshape(
-        count, tail_rows, width
-    )
-    packed = jnp.concatenate([proj_blocks, tail], axis=1).reshape(-1, width)
-    part = lax.psum_scatter(packed, "dp", scatter_dimension=0, tiled=True)
-    total = lax.psum(part, "tm")
+    tail = jnp.pad(tail, ((0, 0), (0, tail_rows * width - tail_cols))).reshape(-1, width)
+    tail_part = lax.psum_scatter(tail, "dp", scatter_dimension=0, tiled=True)
+    total = lax.psum(jnp.concatenate([proj_part, tail_part], axis=0), "tm")
+    proj_rows = proj_part.shape[0]
     proj_total = total[:proj_rows]
     flat_tail = total[proj_rows:].reshape(-1)
     kernel_size = kernel_blocks.shape[1]
     kernel_total = flat_tail[:kernel_size].reshape(-1, kernel_term.shape[1])
     gain_total = flat_tail[kernel_size : kernel_size + gain_blocks.shape[1]]
     return proj_total, kernel_total, gain_total
+
+
+def split_three(values):
+    high = lax.optimization_barrier(values.astype(jnp.bfloat16))
+    rest = values - high.astype(jnp.float32)
+    middle = lax.optimization_barrier(rest.astype(jnp.bfloat16))
+    low = (rest - middle.astype(jnp.float32)).astype(jnp.bfloat16)
+    return jnp.concatenate([high, middle, low], axis=0)
+
+
+def join_three(parts):
+    third = parts.shape[0] // 3
+    wide = parts.astype(jnp.float32)
+    return wide[:third] + wide[third : 2 * third] + wide[2 * third :]
 
 
 def per_device(
@@ -145,105 +156,80 @@
     length = lengths[0]
     full_proj, full_kernel, full_gain = gather_params(projection, kernel, norm_gain)
     query_heads = queries[0].reshape(frame_rows, HEADS, HDIM)
-    key_heads = key_input[0].reshape(frame_rows, HEADS, HDIM)
-    value_heads = value_input[0].reshape(frame_rows, HEADS, HDIM)
-
-    def block_scores(key_block, key_offset):
-        scores = (
-            jnp.einsum("qhd,khd->hqk", query_heads, key_block, preferred_element_type=jnp.float32)
-            * score_scale
-        )
-        key_live = key_offset + jnp.arange(key_block.shape[0], dtype=jnp.int32) < length
-        return jnp.where(key_live[None, None, :], scores, NEG_FILL)
-
-    def absorb(state_now, key_block, value_block, key_offset):
-        run_top, run_total, run_acc = state_now
-        scores = block_scores(key_block, key_offset)
-        new_top = jnp.maximum(run_top, jnp.max(scores, axis=-1))
-        factor = jnp.exp(run_top - new_top)
-        weights = jnp.exp(scores - new_top[:, :, None])
-        run_total = run_total * factor + jnp.sum(weights, axis=-1)
-        contrib = jnp.einsum(
-            "hqk,khd->qhd",
-            weights,
-            value_block.astype(jnp.float32),
-            precision=lax.Precision.HIGHEST,
-        )
-        run_acc = run_acc * jnp.transpose(factor)[:, :, None] + contrib
-        return (new_top, run_total, run_acc)
-
-    start_state = (
-        jnp.full((HEADS, frame_rows), NEG_FILL, jnp.float32),
-        jnp.zeros((HEADS, frame_rows), jnp.float32),
-        jnp.zeros((frame_rows, HEADS, HDIM), jnp.float32),
-    )
-
-    def forward_step(step, loop_state):
-        key_block, value_block, inner = loop_state
-        source = (time_rank - step) % time_count
-        inner = absorb(inner, key_block, value_block, source * frame_rows)
-        key_block, value_block = from_behind((key_block, value_block), "tm", 1)
-        return (key_block, value_block, inner)
-
-    key_block, value_block, inner = lax.fori_loop(
-        0, time_count - 1, forward_step, (key_heads, value_heads, start_state)
-    )
-    source = (time_rank - (time_count - 1)) % time_count
-    state_now = absorb(inner, key_block, value_block, source * frame_rows)
-    run_top, run_total, run_acc = state_now
-    log_total = run_top + jnp.log(run_total)
-    attended = (run_acc / jnp.transpose(run_total)[:, :, None]).astype(jnp.bfloat16)
+    key_own = key_input[0].reshape(frame_rows, HEADS, HDIM)
+    value_own = value_input[0].reshape(frame_rows, HEADS, HDIM)
+    key_value = lax.all_gather(
+        jnp.concatenate([key_input[0], value_input[0]], axis=1), "tm", axis=0, tiled=True
+    )
+    total_frames = key_value.shape[0]
+    key_all = key_value[:, :flat_width].reshape(total_frames, HEADS, HDIM)
+    value_all = key_value[:, flat_width:].reshape(total_frames, HEADS, HDIM)
+    key_live = jnp.arange(total_frames, dtype=jnp.int32) < length
+    scores = (
+        jnp.einsum("qhd,khd->hqk", query_heads, key_all, preferred_element_type=jnp.float32)
+        * score_scale
+    )
+    scores = jnp.where(key_live[None, None, :], scores, NEG_FILL)
+    row_top = jnp.max(scores, axis=-1)
+    log_total = row_top + jnp.log(jnp.sum(jnp.exp(scores - row_top[:, :, None]), axis=-1))
+    weights = jnp.exp(scores - log_total[:, :, None])
+    weights_high = lax.optimization_barrier(weights.astype(jnp.bfloat16))
+    weights_rest = (weights - weights_high.astype(jnp.float32)).astype(jnp.bfloat16)
+    attended = (
+        jnp.einsum("hqk,khd->qhd", weights_high, value_all, preferred_element_type=jnp.float32)
+        + jnp.einsum("hqk,khd->qhd", weights_rest, value_all, preferred_element_type=jnp.float32)
+    ).astype(jnp.bfloat16)
     upstream_rows = upstream[0]
     grad_out = jnp.dot(upstream_rows, full_proj, preferred_element_type=jnp.float32).astype(
         jnp.bfloat16
     )
     grad_heads = grad_out.reshape(frame_rows, HEADS, HDIM)
     row_delta = jnp.einsum("qhd,qhd->hq", grad_heads, attended, preferred_element_type=jnp.float32)
-
-    def backward_block(key_block, value_block, key_offset):
-        scores = block_scores(key_block, key_offset)
-        weights = jnp.exp(scores - log_total[:, :, None])
-        weights_low = weights.astype(jnp.bfloat16)
-        add_value = jnp.einsum(
-            "hqk,qhd->khd", weights_low, grad_heads, preferred_element_type=jnp.float32
-        )
-        grad_weights = jnp.einsum(
-            "qhd,khd->hqk", grad_heads, value_block, preferred_element_type=jnp.float32
-        )
-        grad_scores = (weights * (grad_weights - row_delta[:, :, None]) * score_scale).astype(
-            jnp.bfloat16
-        )
-        add_query = jnp.einsum(
-            "hqk,khd->qhd", grad_scores, key_block, preferred_element_type=jnp.float32
-        )
-        add_key = jnp.einsum(
-            "hqk,qhd->khd", grad_scores, query_heads, preferred_element_type=jnp.float32
-        )
-        return (add_query, add_key, add_value)
-
-    zero_heads = jnp.zeros((frame_rows, HEADS, HDIM), jnp.float32)
-
-    def pass_grads(key_acc, value_acc):
-        return from_behind((key_acc, value_acc), "tm", 1)
-
-    def backward_step(step, loop_state):
-        key_block, value_block, key_acc, value_acc, query_acc = loop_state
-        source = (time_rank - step) % time_count
-        add_query, add_key, add_value = backward_block(key_block, value_block, source * frame_rows)
-        key_acc, value_acc = pass_grads(key_acc + add_key, value_acc + add_value)
-        key_block, value_block = from_behind((key_block, value_block), "tm", 1)
-        return (key_block, value_block, key_acc, value_acc, query_acc + add_query)
-
-    key_block, value_block, key_acc, value_acc, query_acc = lax.fori_loop(
-        0,
-        time_count - 1,
-        backward_step,
-        (key_heads, value_heads, zero_heads, zero_heads, zero_heads),
-    )
-    source = (time_rank - (time_count - 1)) % time_count
-    add_query, add_key, add_value = backward_block(key_block, value_block, source * frame_rows)
-    key_acc, value_acc = pass_grads(key_acc + add_key, value_acc + add_value)
-    query_acc = query_acc + add_query
+    grad_weights = jnp.einsum(
+        "qhd,khd->hqk", grad_heads, value_all, preferred_element_type=jnp.float32
+    )
+    grad_scores = (weights * (grad_weights - row_delta[:, :, None]) * score_scale).astype(
+        jnp.bfloat16
+    )
+    query_acc = jnp.einsum("hqk,khd->qhd", grad_scores, key_all, preferred_element_type=jnp.float32)
+    stat_parts = split_three(jnp.concatenate([log_total, row_delta], axis=0))
+    pair_width = 2 * flat_width
+    stat_rows = -(-stat_parts.size // pair_width)
+    stat_rows = -(-stat_rows // 16) * 16
+    stat_block = jnp.pad(stat_parts.reshape(-1), (0, stat_rows * pair_width - stat_parts.size))
+    packed_rows = jnp.concatenate(
+        [
+            jnp.concatenate([queries[0], grad_out], axis=1),
+            stat_block.reshape(stat_rows, pair_width),
+        ],
+        axis=0,
+    )
+    query_grad = lax.all_gather(packed_rows, "tm", axis=0, tiled=False)
+    query_pairs = query_grad[:, :frame_rows].reshape(total_frames, pair_width)
+    stat_all = query_grad[:, frame_rows:].reshape(time_count, -1)[:, : stat_parts.size]
+    stat_all = stat_all.reshape(time_count, stat_parts.shape[0], frame_rows)
+    stat_all = join_three(jnp.transpose(stat_all, (1, 0, 2)).reshape(stat_parts.shape[0], -1))
+    query_all = query_pairs[:, :flat_width].reshape(total_frames, HEADS, HDIM)
+    grad_all = query_pairs[:, flat_width:].reshape(total_frames, HEADS, HDIM)
+    log_total_all = stat_all[:HEADS]
+    row_delta_all = stat_all[HEADS:]
+    own_live = time_rank * frame_rows + jnp.arange(frame_rows, dtype=jnp.int32) < length
+    scores_k = (
+        jnp.einsum("qhd,khd->hqk", query_all, key_own, preferred_element_type=jnp.float32)
+        * score_scale
+    )
+    scores_k = jnp.where(own_live[None, None, :], scores_k, NEG_FILL)
+    weights_k = jnp.exp(scores_k - log_total_all[:, :, None])
+    value_acc = jnp.einsum(
+        "hqk,qhd->khd", weights_k.astype(jnp.bfloat16), grad_all, preferred_element_type=jnp.float32
+    )
+    grad_weights_k = jnp.einsum(
+        "qhd,khd->hqk", grad_all, value_own, preferred_element_type=jnp.float32
+    )
+    grad_scores_k = (
+        weights_k * (grad_weights_k - row_delta_all[:, :, None]) * score_scale
+    ).astype(jnp.bfloat16)
+    key_acc = jnp.einsum("hqk,qhd->khd", grad_scores_k, query_all, preferred_element_type=jnp.float32)
     grad_queries = query_acc.reshape(1, frame_rows, flat_width).astype(jnp.bfloat16)
     grad_keys = key_acc.reshape(1, frame_rows, flat_width).astype(jnp.bfloat16)
     grad_values = value_acc.reshape(1, frame_rows, flat_width).astype(jnp.bfloat16)

time: 667 us -> 658 us (0.987)
  waiting for transfers between devices: 248 us -> 345 us
  starting transfers between devices: 54 us -> 12.6 us
  local copies, waits for them, and re-layouts: 116 us -> 78.7 us
  matrix products: 76.7 us -> 42 us
    ppermute x44 -> x0, waiting for transfers between devices: 179 us -> none  [from_behind(): return lax.ppermute(block, axis, route)]
    reduce_scatter x1, waiting for transfers between devices: 0.01 us -> 108 us  [reduce_grads(): lax.psum_scatter(proj_term, 'dp', scatter_dimension=0, tiled=True)]
    all_gather x0 -> x2, waiting for transfers between devices: none -> 65.5 us  [the longest x1 65.5 us: per_device(): query_grad = lax.all_gather(packed_rows, 'tm', axis=0, tiled=False)]
    all_gather x1, waiting for transfers between devices: 0.01 us -> 62.8 us  [gather_params(): full = lax.all_gather(block, 'dp', axis=0, tiled=False)]
    ppermute x44 -> x0, starting transfers between devices: 44.6 us -> none  [from_behind(): return lax.ppermute(block, axis, route)]
    dot_general x56 -> x7, matrix products: 73.4 us -> 35.8 us  [the longest x1 8.78 us: per_device(): jnp.einsum('hqk,khd->qhd', grad_scores, key_all, preferred_element_type=j...]
    unnamed x3 -> x7, waiting for transfers between devices: 0.05 us -> 36.2 us
    while x38 -> x0, local copies, waits for them, and re-layouts: 27.7 us -> none
  transfers between devices with their start and end apart: 51 -> 10, of which waited for: 30 -> 6; matrix products, arithmetic and copies ran while one was open for 31% -> 40% of each run, Pallas kernels for 0% -> 0%
where the time goes in v2:
time: 658 us; the launch traced here: 646 us
  waiting for transfers between devices  345 us (52%)
  other arithmetic  151 us (23%)
  local copies, waits for them, and re-layouts  78.7 us (12%)
  matrix products  42 us (6%)
  between operations  16.7 us (3%)
  starting transfers between devices  12.6 us (2%)
    reduce_scatter x1, waiting for transfers between devices, reduce_grads(): lax.psum_scatter(proj_term, 'dp', scatter_dimension=0, tiled=True)  108 us
    psum x1, waiting for transfers between devices, reduce_grads(): total = lax.psum(jnp.concatenate([proj_part, tail_part], axis=0), 'tm')  71.1 us
    all_gather x1, waiting for transfers between devices, per_device(): query_grad = lax.all_gather(packed_rows, 'tm', axis=0, tiled=False)  65.5 us
    all_gather x1, waiting for transfers between devices, gather_params(): full = lax.all_gather(block, 'dp', axis=0, tiled=False)  62.8 us
    reduce_sum x4, other arithmetic, tap_products(): jnp.sum(grad_f * padded[tap:tap + frame_rows].astype(jnp.float32), axis=0)  47.2 us
    reduce_sum x1, other arithmetic, norm_backward(): centre = mixed - jnp.mean(mixed, axis=-1, keepdims=True)  45.4 us
    unnamed x7, waiting for transfers between devices  36.2 us
    concatenate x3, other arithmetic, per_device(): jnp.concatenate([first_half, second_half], axis=-1).astype(jnp.bfloat16)  36.1 us
  transfers between devices with their start and end apart: 10, of which 6 were waited for; matrix products, arithmetic and copies ran while one was open for 40% of the time, Pallas kernels for 0%

profile of v2, /device:TPU:4, one launch (start us, length us, event | category | flops | bytes accessed | tf_op | source)
XLA Modules:
  0.0 645.9 jit_solution(10095219337731439933)
XLA Ops:
  9.1 1.5 pad_maximum_fusion.9
  11.8 2.9 fusion.11
  18.0 5.2 collective-permute-start
  23.2 1.7 copy.82
  25.7 1.8 pad_maximum_fusion.6
  29.2 62.8 %all-gather.8.cloned.1.call-done = bf16[4352,256]{1,0:T(8,128)(2,1)} async-done(((bf16[136,256]{1,0:T(8,128)(2,1)}), bf16[4352,256]{1,0:T(8,128)(2,1)}) %all-gather.8.cloned.1.call-update) | async-done | bytes 2228240 | tf_op jit(solution)/shard_map/all_gather | solution.py:93
  92.9 2.2 reshape.264
  95.2 19.6 %slice_reduce_fusion.30 = (f32[2048]{0:T(1024)S(1)}, f32[2048]{0:T(1024)S(1)}, f32[2048]{0:T(1024)S(1)}, f32[2048]{0:T(1024)S(1)}, f32[2048]{0:T(1024)S(1)}, /*i...) fusion(f32[2048,31]{1,0:T(8,128)} %reshape.264), kind=kLoop, calls=%fused_computation.353 | loop fusion | bytes 311296 | tf_op jit(solution)/shard_map/slice | solution.py:42
  114.9 6.6 %slice_reduce_fusion.29 = (f32[2048]{0:T(1024)S(1)}, f32[2048]{0:T(1024)S(1)}, f32[2048]{0:T(1024)S(1)}, f32[2048]{0:T(1024)S(1)}, f32[2048]{0:T(1024)S(1)}, /*i...) fusion(f32[2048,31]{1,0:T(8,128)S(1)} %copy-done.2), kind=kLoop, calls=%fused_computation.352 | loop fusion | bytes 196608 | tf_op jit(solution)/shard_map/slice | solution.py:42
  122.3 1.6 slice.602
  124.2 45.4 %fusion.185 = (f32[384]{0:T(512)S(1)}, f32[384,2048]{1,0:T(8,128)S(1)}) fusion(f32[2048]{0:T(1024)S(1)} %get-tuple-element.70, bf16[15,2048]{1,0:T(8,128)(2,1)} %collective-permute-done.1, bf16[384,2048]{1,0:T(8,128)(2,1)} %copy-done.4, f32[2048]{0:T(1024)S(1)} %get-tuple-element.71, f32[2048]{0:T(1024)S(1)} %get-tuple-element.72, ...), kind=kLoop, calls=%fused_computation.397 | loop fusion | flops 143916672 | bytes 5096960 | tf_op jit(solution)/shard_map/reduce_sum | solution.py:69
  170.2 3.9 multiply_reduce_fusion.1
  174.2 20.4 %fusion.75 = (f32[2048]{0:T(1024)}, f32[2048]{0:T(1024)}, f32[2048]{0:T(1024)}, f32[2048]{0:T(1024)}, f32[2048]{0:T(1024)}, /*index=5*/f32[2048]{0:T(1024)}, f32...) fusion(bf16[15,2048]{1,0:T(8,128)(2,1)} %collective-permute-done.1, ...), kind=kLoop, calls=%fused_computation.204 | loop fusion | flops 49526784 | bytes 9586688 | tf_op jit(solution)/shard_map/reduce_sum | solution.py:61
  194.6 4.2 fusion.58
  198.8 15.3 %fusion.74 = (f32[2048]{0:T(1024)S(1)}, f32[2048]{0:T(1024)S(1)}, f32[2048]{0:T(1024)S(1)}, f32[2048]{0:T(1024)S(1)}, f32[2048]{0:T(1024)S(1)}, /*index=5*/f32[2048]{0:T(1024)S(1)}, f32[2048]{0:T(1024)S(1)}) fusion(bf16[384,2048]{1,0:T(8,128)(2,1)S(1)} %get-tuple-element.102, bf16[15,2048]{1,0:T(8,128)(2,1)} %collective-permute-done.1, ...), kind=kLoop, calls=%fused_computation.203 | loop fusion | flops 31442944 | bytes 3264512 | tf_op jit(solution)/shard_map/reduce_sum | solution.py:61
  214.1 7.3 %fusion.59 = (f32[2048]{0:T(1024)S(1)}, f32[2048]{0:T(1024)}, f32[2048]{0:T(1024)}, f32[2048]{0:T(1024)}, f32[2048]{0:T(1024)}, /*index=5*/f32[2048]{0:T(1024)}, f32[2048]{0:T(1024)}, f32[2048]{0:T(1024)}, f32[2048]{0:T(1024)}) fusion(bf16[384,2048]{1,0:T(8,128)(2,1)S(1)} %get-tuple-element.102, bf16[384,2048]{1,0:T(8,128)(2,1)S(1)} %copy-done.5, ...), kind=kLoop, calls=%fused_computation.188 | loop fusion | flops 43235328 | bytes 3280896 | tf_op jit(solution)/shard_map/reduce_sum | solution.py:61
  221.4 3.4 stack.127
  226.2 1.7 reshape.259
  228.7 1.7 reshape.273
  230.4 2.9 fusion.160
  233.4 2.1 fusion.189
  235.5 2.6 bitcast_reduce_fusion
  238.2 2.2 fusion.1
  240.4 2.1 fusion.4
  242.5 3.2 fusion.7
  253.4 1.8 pad_maximum_fusion.5
  255.2 2.0 copy.94
  257.3 1.7 reshape_squeeze.10
  259.0 1.7 reshape_squeeze.11
  260.6 1.5 fusion.190
  262.2 4.6 collective-permute-start.3
  268.0 3.3 convolution_bitcast_fusion
  273.5 33.0 %fusion.97 = (bf16[1,384,2048]{2,1,0:T(8,128)(2,1)S(1)}, f32[384,2048]{1,0:T(8,128)S(1)}) fusion(bf16[384,4096]{1,0:T(8,128)(2,1)} %bitcast.138, f32[384]{0:T(512)S(1)} %copy-done.86, f32[2048]{0:T(1024)S(1)} %copy-done.23, bf16[384,2048]{1,0:T(8,128)(2,1)S(1)} %copy-done.8, bf16[15,2048]{1,0:T(8,128)(2,1)} %collective-permute-done.3, ...), kind=kLoop, calls=%fused_computation.236 | loop fusion | flops 148635648 | bytes 8242688 | tf_op jit(solution)/shard_map/concatenate | solution.py:253
  307.7 2.0 pad_maximum_fusion
  309.7 36.1 %reduce-scatter.7.cloned.1.call-done = f32[8,256]{1,0:T(8,128)} async-done(((f32[256,256]{1,0:T(8,128)}), f32[8,256]{1,0:T(8,128)}) %reduce-scatter.7.cloned.1.call-update) | async-done | bytes 8208
  346.6 8.8 %fusion.158 = bf16[2,128,384]{2,1,0:T(8,128)(2,1)} fusion(bf16[3072,2,128]{0,2,1:T(8,128)(2,1)S(1)} %bitcast.142, bf16[384,2,128]{0,2,1:T(8,128)(2,1)S(1)} %bitcast.156, bf16[3072,2,128]{0,2,1:T(8,128)(2,1)S(1)} %bitcast.145, f32[2,3072,384]{2,1,0:T(8,128)} %copy-done.3, f32[2,384]{1,0:T(2,128)S(1)} %copy-done.84, f32[2,384]{1,0:T(2,128)S(1)} %log_add_fusion, ...), kind=kOutput, calls=%fused_computation.319 | convolution fusion | flops 1224572928 | bytes 12985344 | tf_op jit(solution)/shard_map/hqk,khd->qhd/dot_general | solution.py:194
  355.4 1.7 copy.104
  357.2 65.5 %all-gather.10.cloned.1.call-done = bf16[3200,512]{1,0:T(8,128)(2,1)} async-done(((bf16[400,512]{1,0:T(8,128)(2,1)}), bf16[3200,512]{1,0:T(8,128)(2,1)}) %all-gather.10.cloned.1.call-update) | async-done | bytes 3276816 | tf_op jit(solution)/shard_map/all_gather | solution.py:207
  422.7 2.1 slice.604
  424.8 1.9 fusion.188
  426.6 1.8 copy.127
  428.5 2.0 copy.128
  431.7 5.2 fusion.169
  436.9 8.5 %fusion.157 = bf16[2,128,384]{2,1,0:T(8,128)(2,1)S(1)} fusion(bf16[3072,2,128]{0,2,1:T(8,128)(2,1)S(1)} %bitcast.147, f32[2,3072,384]{2,1,0:T(8,128)} %fusion.169, bf16[3072,2,128]{0,2,1:T(8,128)(2,1)S(1)} %bitcast.154, f32[2,3072]{1,0:T(2,128)S(1)} %bitcast.205, f32[2,3072]{1,0:T(2,128)S(1)} %bitcast.203, pred[384]{0:T(512)(128)(4,1)S(1)} %copy-done.88, ...), kind=kOutput, calls=%fused_computation.318 | convolution fusion | flops 1224572928 | bytes 13025664 | tf_op jit(solution)/shard_map/hqk,qhd->khd/dot_general | solution.py:232
  445.4 108.3 %reduce-scatter.5.cloned.1.call-done = f32[128,256]{0,1:T(8,128)} async-done(((f32[4096,256]{0,1:T(8,128)}), f32[128,256]{0,1:T(8,128)}) %reduce-scatter.5.cloned.1.call-update) | async-done | bytes 131088 | tf_op jit(solution)/shard_map/reduce_scatter | solution.py:107
  553.7 1.6 pad_maximum_fusion.8
  555.4 6.5 fusion.163
  563.5 71.1 %all-reduce.3.cloned.1.call-done = f32[136,256]{0,1:T(8,128)} async-done(((f32[136,256]{0,1:T(8,128)}), f32[136,256]{0,1:T(8,128)}) %all-reduce.3.cloned.1.call-update) | async-done | bytes 139280 | tf_op jit(solution)/shard_map/psum | solution.py:115
  (249 shorter events, 32.2 us)
Async XLA Ops:
  7.2 223.2 %copy-start = (bf16[1,384,4096]{2,1,0:T(8,128)(2,1)S(1)}, bf16[1,384,4096]{2,1,0:T(8,128)(2,1)}, u32[]{:S(2)}) copy-start(bf16[1,384,4096]{2,1,0:T(8,128)(2,1)} %param.15) | copy-start | bytes 9437188
  7.2 17.7 %copy-start.19 = (bf16[1,384,256]{2,1,0:T(8,128)(2,1)S(1)}, bf16[1,384,256]{2,1,0:T(8,128)(2,1)}, u32[]{:S(2)}) copy-start(bf16[1,384,256]{2,1,0:T(8,128)(2,1)} %param.11) | copy-start | bytes 589828
  7.2 84.8 %all-gather.8.cloned.1.call-start = ((), (), s32[]{:S(2)}) async-start(), calls=%async_computation.5 | async-start | bytes 2297856 | tf_op jit(solution)/shard_map/all_gather | solution.py:93
  10.6 222.8 %all-gather.6.cloned.1.call-start = ((), (), s32[]{:S(2)}) async-start(), calls=%async_computation.2 | async-start | bytes 3538944 | tf_op jit(solution)/shard_map/all_gather | solution.py:161
  11.8 158.3 %copy-start.85 = (f32[384]{0:T(512)}, f32[384]{0:T(512)S(1)}, u32[]{:S(2)}) copy-start(f32[384]{0:T(512)S(1)} %get-tuple-element.106) | copy-start | bytes 4612
  11.8 15.8 %copy-start.18 = (bf16[1,384,256]{2,1,0:T(8,128)(2,1)S(1)}, bf16[1,384,256]{2,1,0:T(8,128)(2,1)}, u32[]{:S(2)}) copy-start(bf16[1,384,256]{2,1,0:T(8,128)(2,1)} %param.10) | copy-start | bytes 589828
  16.7 107.3 %collective-permute-start.1 = (bf16[15,2048]{1,0:T(8,128)(2,1)}, bf16[15,2048]{1,0:T(8,128)(2,1)}, u32[]{:S(2)}, u32[]{:S(2)}) collective-permute-start(bf16[15,2048]{1,0:T(8,128)(2,1)} %get-tuple-element.115), channel_id=1, source_target_pairs={{1,0},{2,1},{3,2},{4,3},{5,4},{6,5},{7,6},{9,8},{10,9},{11,10},{12... | collective-permute-start | bytes 184328 | tf_op jit(solution)/shard_map/ppermute | solution.py:32
  18.0 106.0 %collective-permute-start = (bf16[15,2048]{1,0:T(8,128)(2,1)}, bf16[15,2048]{1,0:T(8,128)(2,1)}, u32[]{:S(2)}, u32[]{:S(2)}) collective-permute-start(bf16[15,2048]{1,0:T(8,128)(2,1)} %get-tuple-element.114), channel_id=1, source_target_pairs={{0,1},{1,2},{2,3},{3,4},{4,5},{5,6},{6,7},{8,9},{9,10},{10,11},{11... | collective-permute-start | bytes 184328 | tf_op jit(solution)/shard_map/ppermute | solution.py:30
  27.6 318.2 %reduce-scatter.7.cloned.1.call-start = ((), (), s32[]{:S(2)}) async-start(), calls=%async_computation.7 | async-start | bytes 270336
  95.2 19.6 %copy-start.2 = (f32[2048,31]{1,0:T(8,128)S(1)}, f32[2048,31]{1,0:T(8,128)}, u32[]{:S(2)}) copy-start(f32[2048,31]{1,0:T(8,128)} %reshape.264) | copy-start | bytes 761860
  114.8 9.2 %copy-start.22 = (f32[2048]{0:T(1024)}, f32[2048]{0:T(1024)S(1)}, u32[]{:S(2)}) copy-start(f32[2048]{0:T(1024)S(1)} %get-tuple-element.70) | copy-start | bytes 24580
  114.8 9.2 %copy-start.24 = (f32[2048]{0:T(1024)}, f32[2048]{0:T(1024)S(1)}, u32[]{:S(2)}) copy-start(f32[2048]{0:T(1024)S(1)} %get-tuple-element.71) | copy-start | bytes 24580
  114.8 9.2 %copy-start.26 = (f32[2048]{0:T(1024)}, f32[2048]{0:T(1024)S(1)}, u32[]{:S(2)}) copy-start(f32[2048]{0:T(1024)S(1)} %get-tuple-element.72) | copy-start | bytes 24580
  114.8 9.2 %copy-start.28 = (f32[2048]{0:T(1024)}, f32[2048]{0:T(1024)S(1)}, u32[]{:S(2)}) copy-start(f32[2048]{0:T(1024)S(1)} %get-tuple-element.73) | copy-start | bytes 24580
  114.8 9.2 %copy-start.30 = (f32[2048]{0:T(1024)}, f32[2048]{0:T(1024)S(1)}, u32[]{:S(2)}) copy-start(f32[2048]{0:T(1024)S(1)} %get-tuple-element.74) | copy-start | bytes 24580
  114.8 9.2 %copy-start.32 = (f32[2048]{0:T(1024)}, f32[2048]{0:T(1024)S(1)}, u32[]{:S(2)}) copy-start(f32[2048]{0:T(1024)S(1)} %get-tuple-element.75) | copy-start | bytes 24580
  114.8 9.2 %copy-start.34 = (f32[2048]{0:T(1024)}, f32[2048]{0:T(1024)S(1)}, u32[]{:S(2)}) copy-start(f32[2048]{0:T(1024)S(1)} %get-tuple-element.76) | copy-start | bytes 24580
  114.8 9.2 %copy-start.36 = (f32[2048]{0:T(1024)}, f32[2048]{0:T(1024)S(1)}, u32[]{:S(2)}) copy-start(f32[2048]{0:T(1024)S(1)} %get-tuple-element.77) | copy-start | bytes 24580
  114.8 9.2 %copy-start.38 = (f32[2048]{0:T(1024)}, f32[2048]{0:T(1024)S(1)}, u32[]{:S(2)}) copy-start(f32[2048]{0:T(1024)S(1)} %get-tuple-element.78) | copy-start | bytes 24580
  114.8 9.2 %copy-start.40 = (f32[2048]{0:T(1024)}, f32[2048]{0:T(1024)S(1)}, u32[]{:S(2)}) copy-start(f32[2048]{0:T(1024)S(1)} %get-tuple-element.79) | copy-start | bytes 24580
  114.9 9.2 %copy-start.42 = (f32[2048]{0:T(1024)}, f32[2048]{0:T(1024)S(1)}, u32[]{:S(2)}) copy-start(f32[2048]{0:T(1024)S(1)} %get-tuple-element.80) | copy-start | bytes 24580
  114.9 9.2 %copy-start.44 = (f32[2048]{0:T(1024)}, f32[2048]{0:T(1024)S(1)}, u32[]{:S(2)}) copy-start(f32[2048]{0:T(1024)S(1)} %get-tuple-element.81) | copy-start | bytes 24580
  121.5 48.1 %copy-start.58 = (f32[2048]{0:T(1024)}, f32[2048]{0:T(1024)S(1)}, u32[]{:S(2)}) copy-start(f32[2048]{0:T(1024)S(1)} %get-tuple-element.88) | copy-start | bytes 24580
  121.5 48.1 %copy-start.60 = (f32[2048]{0:T(1024)}, f32[2048]{0:T(1024)S(1)}, u32[]{:S(2)}) copy-start(f32[2048]{0:T(1024)S(1)} %get-tuple-element.89) | copy-start | bytes 24580
  121.5 48.1 %copy-start.62 = (f32[2048]{0:T(1024)}, f32[2048]{0:T(1024)S(1)}, u32[]{:S(2)}) copy-start(f32[2048]{0:T(1024)S(1)} %get-tuple-element.90) | copy-start | bytes 24580
  121.5 48.1 %copy-start.64 = (f32[2048]{0:T(1024)}, f32[2048]{0:T(1024)S(1)}, u32[]{:S(2)}) copy-start(f32[2048]{0:T(1024)S(1)} %get-tuple-element.91) | copy-start | bytes 24580
  121.6 48.1 %copy-start.66 = (f32[2048]{0:T(1024)}, f32[2048]{0:T(1024)S(1)}, u32[]{:S(2)}) copy-start(f32[2048]{0:T(1024)S(1)} %get-tuple-element.92) | copy-start | bytes 24580
  121.6 48.1 %copy-start.68 = (f32[2048]{0:T(1024)}, f32[2048]{0:T(1024)S(1)}, u32[]{:S(2)}) copy-start(f32[2048]{0:T(1024)S(1)} %get-tuple-element.93) | copy-start | bytes 24580
  121.6 48.1 %copy-start.70 = (f32[2048]{0:T(1024)}, f32[2048]{0:T(1024)S(1)}, u32[]{:S(2)}) copy-start(f32[2048]{0:T(1024)S(1)} %get-tuple-element.94) | copy-start | bytes 24580
  121.6 48.1 %copy-start.72 = (f32[2048]{0:T(1024)}, f32[2048]{0:T(1024)S(1)}, u32[]{:S(2)}) copy-start(f32[2048]{0:T(1024)S(1)} %get-tuple-element.95) | copy-start | bytes 24580
  121.6 48.1 %copy-start.74 = (f32[2048]{0:T(1024)}, f32[2048]{0:T(1024)S(1)}, u32[]{:S(2)}) copy-start(f32[2048]{0:T(1024)S(1)} %get-tuple-element.96) | copy-start | bytes 24580
  121.6 48.1 %copy-start.76 = (f32[2048]{0:T(1024)}, f32[2048]{0:T(1024)S(1)}, u32[]{:S(2)}) copy-start(f32[2048]{0:T(1024)S(1)} %get-tuple-element.97) | copy-start | bytes 24580
  121.6 48.1 %copy-start.78 = (f32[2048]{0:T(1024)}, f32[2048]{0:T(1024)S(1)}, u32[]{:S(2)}) copy-start(f32[2048]{0:T(1024)S(1)} %get-tuple-element.98) | copy-start | bytes 24580
  121.6 48.1 %copy-start.80 = (f32[2048]{0:T(1024)}, f32[2048]{0:T(1024)S(1)}, u32[]{:S(2)}) copy-start(f32[2048]{0:T(1024)S(1)} %get-tuple-element.99) | copy-start | bytes 24580
  124.2 46.0 %copy-start.16 = (bf16[1,384,2048]{2,1,0:T(8,128)(2,1)S(1)}, bf16[1,384,2048]{2,1,0:T(8,128)(2,1)}, u32[]{:S(2)}) copy-start(bf16[1,384,2048]{2,1,0:T(8,128)(2,1)} %param.19) | copy-start | bytes 4718596
  174.2 20.4 %copy-start.5 = (bf16[384,2048]{1,0:T(8,128)(2,1)S(1)}, bf16[384,2048]{1,0:T(8,128)(2,1)}, u32[]{:S(2)}) copy-start(bf16[384,2048]{1,0:T(8,128)(2,1)} %copy-done.4) | copy-start | bytes 4718596
  194.6 19.5 %copy-start.7 = (bf16[384,2048]{1,0:T(8,128)(2,1)}, bf16[384,2048]{1,0:T(8,128)(2,1)S(1)}, u32[]{:S(2)}) copy-start(bf16[384,2048]{1,0:T(8,128)(2,1)S(1)} %get-tuple-element.102) | copy-start | bytes 4718596
  233.3 189.4 %all-gather.10.cloned.1.call-start = ((), (), s32[]{:S(2)}) async-start(), calls=%async_computation.6 | async-start | bytes 3686400 | tf_op jit(solution)/shard_map/all_gather | solution.py:207
  235.5 10.2 %copy-start.13 = (bf16[3072,256]{0,1:T(8,128)(2,1)}, bf16[3072,256]{0,1:T(8,128)(2,1)S(1)}, u32[]{:S(2)}) copy-start(bf16[3072,256]{0,1:T(8,128)(2,1)S(1)} %get-tuple-element.110) | copy-start | bytes 4718596
  257.2 296.5 %reduce-scatter.5.cloned.1.call-start = ((), (), s32[]{:S(2)}) async-start(), calls=%async_computation.3 | async-start | bytes 4325376 | tf_op jit(solution)/shard_map/reduce_scatter | solution.py:107
  262.2 9.6 %collective-permute-start.3 = (bf16[15,2048]{1,0:T(8,128)(2,1)}, bf16[15,2048]{1,0:T(8,128)(2,1)}, u32[]{:S(2)}, u32[]{:S(2)}) collective-permute-start(bf16[15,2048]{1,0:T(8,128)(2,1)} %get-tuple-element.113), channel_id=1, source_target_pairs={{0,1},{1,2},{2,3},{3,4},{4,5},{5,6},{6,7},{8,9},{9,10},{10,11},{11... | collective-permute-start | bytes 184328 | tf_op jit(solution)/shard_map/ppermute | solution.py:30
  266.7 6.5 %collective-permute-start.2 = (bf16[15,2048]{1,0:T(8,128)(2,1)}, bf16[15,2048]{1,0:T(8,128)(2,1)}, u32[]{:S(2)}, u32[]{:S(2)}) collective-permute-start(bf16[15,2048]{1,0:T(8,128)(2,1)} %get-tuple-element.112), channel_id=1, source_target_pairs={{1,0},{2,1},{3,2},{4,3},{5,4},{6,5},{7,6},{9,8},{10,9},{11,10},{12... | collective-permute-start | bytes 184328 | tf_op jit(solution)/shard_map/ppermute | solution.py:32
  271.7 362.9 %all-reduce.3.cloned.1.call-start = ((), (), s32[]{:S(2)}) async-start(), calls=%async_computation.4 | async-start | bytes 524288 | tf_op jit(solution)/shard_map/psum | solution.py:115
  271.7 34.8 %copy-start.9 = (bf16[1,384,4096]{2,1,0:T(8,128)(2,1)S(1)}, bf16[1,384,4096]{2,1,0:T(8,128)(2,1)}, u32[]{:S(2)}) copy-start(bf16[1,384,4096]{2,1,0:T(8,128)(2,1)} %param.16) | copy-start | bytes 9437188
  307.6 39.0 %copy-start.11 = (bf16[3072,256]{0,1:T(8,128)(2,1)S(1)}, bf16[3072,256]{0,1:T(8,128)(2,1)}, u32[]{:S(2)}) copy-start(bf16[3072,256]{0,1:T(8,128)(2,1)} %copy-done.10) | copy-start | bytes 4718596
  307.7 39.0 %copy-start.14 = (bf16[3072,256]{0,1:T(8,128)(2,1)S(1)}, bf16[3072,256]{0,1:T(8,128)(2,1)}, u32[]{:S(2)}) copy-start(bf16[3072,256]{0,1:T(8,128)(2,1)} %copy-done.13) | copy-start | bytes 4718596
  307.7 39.0 %copy-start.84 = (f32[2,384]{1,0:T(2,128)S(1)}, f32[2,384]{1,0:T(2,128)}, u32[]{:S(2)}) copy-start(f32[2,384]{1,0:T(2,128)} %copy-done.83) | copy-start | bytes 9220
  555.4 83.3 %copy-start.1 = (bf16[1,384,4096]{2,1,0:T(8,128)(2,1)S(1)}, bf16[1,384,4096]{2,1,0:T(8,128)(2,1)}, u32[]{:S(2)}) copy-start(bf16[1,384,4096]{2,1,0:T(8,128)(2,1)} %param.15) | copy-start | bytes 9437188
  (51 other events, 161.8 us)
Sparse Core Ops, SparseCore 0:
  11.3 80.6 all-gather.7
  93.8 73.0 all-gather.5
  233.4 112.3 reduce-scatter.6
  347.4 75.2 all-gather.9
  426.7 126.9 reduce-scatter.4
  556.2 78.3 all-reduce.2
